TPU v7x, 768 devices: a whole 4x8x12 slice. The times are simulated.
768 devices in a mesh: ctx: 32 (over y, z_hi), tp: 24 (over z_lo, x, core).
Axes of the slice: x: 4, y: 8, z: 12 (z_hi: 4, z_lo: 3; z = z_hi * 3 + z_lo), core: 2. Of those that a mesh axis runs over, the one named last changes fastest.
Arguments:
- tokens: bfloat16 [16384, 5376], P('ctx'), may hold values from -36 to 36, as said below
- norm_gain: float32 [5376], replicated, may hold values from 0.5 to 1.5
- query_weight: bfloat16 [5376, 3072], P(None, 'tp'), may hold values from -0.078125 to 0.078125
- keyval_weight: bfloat16 [5376, 3072], P(None, 'tp'), may hold values from -0.07637626 to 0.07637626
- query_gain: float32 [128], replicated, may hold values from 0.5 to 40
- key_gain: float32 [128], replicated, may hold values from 0.5 to 40
- out_weight: bfloat16 [3072, 5376], P('tp'), may hold values from -2.8 to 2.8
- post_gain: float32 [5376], P('tp'), may hold values from 0.5 to 1.5
Outputs:
- layer_out: bfloat16 [16384, 5376], P('ctx', 'tp')
Inputs may be any that keep to these rules, and one draw needn't show every extreme that they name: `tokens`: each row and feature has its own scale.
All inputs are finite; a program needn't handle non-finite values.
Results may differ from a plain program's by a relative error of at most 0.03.
Values may be sent and summed in bfloat16 or wider, within the bound.
No kernel may reach another device: no remote copies, remote signals or barrier semaphores. Data moves between devices by JAX's collectives and lax.ppermute only.
A program may use at most 128 MiB of HBM per device.

v0:
```python
import jax
import jax.numpy as jnp
from jax import lax
from jax.sharding import Mesh, PartitionSpec as P

WIN = 1024


epsilon = 1e-06
query_scalar = 168.0
rope_base = 10000.0

TP_AXES = ("zl", "x", "core")
Z_HI = 4


def from_behind(block, axis, distance):
    devices = range(lax.axis_size(axis))
    route = [(i - distance, i) for i in devices if i - distance in devices]
    return lax.ppermute(block, axis, route)


def rope_tables(positions, head_width):
    half_width = head_width // 2
    exponent = jnp.arange(half_width, dtype=jnp.float32) * (2.0 / head_width)
    frequency = rope_base ** (-exponent)
    angles = positions.astype(jnp.float32)[:, None] * frequency[None, :]
    cosine = jnp.concatenate([jnp.cos(angles), jnp.cos(angles)], axis=1)
    sine_table = jnp.concatenate([jnp.sin(angles), jnp.sin(angles)], axis=1)
    return (cosine, sine_table)


def rotate(signal, cosine, sine_table):
    half_width = signal.shape[-1] // 2
    turned = jnp.concatenate([-signal[:, half_width:], signal[:, :half_width]], axis=1)
    return signal * cosine + turned * sine_table


def rms_scale(signal, gain_vector):
    return (
        signal
        * lax.rsqrt(jnp.mean(signal * signal, axis=-1, keepdims=True) + epsilon)
        * gain_vector
    )


def layer(
    tokens, norm_gain, query_weight, keyval_weight, query_gain, key_gain, out_weight, post_gain
):
    tok_rows = tokens.shape[0]
    model_width = tokens.shape[1]
    head_width = query_weight.shape[1]
    col_share = post_gain.shape[0]
    n_zl = lax.axis_size("zl")
    n_x = lax.axis_size("x")
    n_core = lax.axis_size("core")
    ctx_index = lax.axis_index("ctx")
    core_index = lax.axis_index("core")
    tp_index = (lax.axis_index("zl") * n_x + lax.axis_index("x")) * n_core + core_index
    is_even = core_index == 0

    as_float = tokens.astype(jnp.float32)
    normed = rms_scale(as_float, norm_gain).astype(jnp.bfloat16)
    positions = ctx_index * tok_rows + jnp.arange(tok_rows, dtype=jnp.int32)
    cosine, sine_table = rope_tables(positions, head_width)

    projected = jnp.dot(normed, keyval_weight, preferred_element_type=jnp.float32)
    rotated = rotate(rms_scale(projected, key_gain), cosine, sine_table)
    own_block = jnp.where(is_even, rotated, projected).astype(jnp.bfloat16)
    n_tp = n_zl * n_x * n_core
    weight_block = lax.all_to_all(
        out_weight.reshape(head_width, n_tp, col_share), TP_AXES, 1, 0, tiled=True
    ).reshape(n_tp * head_width, col_share)
    span_count = WIN // tok_rows
    n_ctx = lax.axis_size("ctx")
    devices = range(n_ctx)
    mid = [(c // Z_HI) * Z_HI + (c % Z_HI - 1) % Z_HI for c in devices]
    first_leg = [(c, mid[c]) for c in devices if c + span_count in devices]
    second_leg = [(mid[c], c + span_count) for c in devices if c + span_count in devices]
    far_block = lax.ppermute(lax.ppermute(own_block, "ctx", first_leg), "ctx", second_leg)
    earlier = [far_block] + [
        from_behind(own_block, "ctx", offset) for offset in range(span_count - 1, 0, -1)
    ]
    own_window = jnp.concatenate(earlier + [own_block], axis=0)
    other_window = lax.ppermute(own_window, "core", [(0, 1), (1, 0)])
    weight_block, own_window, other_window = lax.optimization_barrier(
        (weight_block, own_window, other_window)
    )
    key_window = jnp.where(is_even, own_window, other_window)
    value_window = jnp.where(is_even, other_window, own_window)

    queries = jnp.dot(normed, query_weight, preferred_element_type=jnp.float32)
    queries = (
        rotate(rms_scale(queries, query_gain), cosine, sine_table) * query_scalar ** (-0.5)
    ).astype(jnp.bfloat16)

    key_pos = ctx_index * tok_rows - WIN + jnp.arange(WIN + tok_rows, dtype=jnp.int32)
    distance = positions[:, None] - key_pos[None, :]
    allowed = (key_pos[None, :] >= 0) & (distance >= 0) & (distance < WIN)
    scores = lax.dot_general(
        queries,
        key_window,
        (((1,), (1,)), ((), ())),
        preferred_element_type=jnp.float32,
    )
    scores = jnp.where(allowed, scores, -1e30)
    row_max = jnp.max(scores, axis=1, keepdims=True)
    lifted = jnp.exp(scores - row_max)
    weights = (lifted / jnp.sum(lifted, axis=1, keepdims=True)).astype(jnp.bfloat16)
    attended = jnp.dot(weights, value_window, preferred_element_type=jnp.float32).astype(
        jnp.bfloat16
    )

    n_peer = n_zl * n_x
    copies = jnp.broadcast_to(attended[None], (n_peer,) + attended.shape)
    own_heads = lax.all_to_all(copies, ("zl", "x"), 0, 0, tiled=True)
    other_heads = lax.ppermute(own_heads, "core", [(0, 1), (1, 0)])
    rows = weight_block.reshape(n_peer, n_core, head_width, col_share)
    own_rows = jnp.where(is_even, rows[:, 0], rows[:, 1])
    other_rows = jnp.where(is_even, rows[:, 1], rows[:, 0])
    contract = (((0, 2), (0, 1)), ((), ()))
    summed = lax.dot_general(
        own_heads, own_rows, contract, preferred_element_type=jnp.float32
    ) + lax.dot_general(other_heads, other_rows, contract, preferred_element_type=jnp.float32)
    squares = jnp.sum(summed * summed, axis=1)
    square_copies = jnp.broadcast_to(squares[None], (n_tp,) + squares.shape)
    squares = jnp.sum(lax.all_to_all(square_copies, TP_AXES, 0, 0, tiled=True), axis=0)
    scaled = summed * lax.rsqrt(squares[:, None] / model_width + epsilon) * post_gain
    residual = lax.dynamic_slice_in_dim(tokens, tp_index * col_share, col_share, 1)
    return (residual.astype(jnp.float32) + scaled).astype(jnp.bfloat16)


def solution(mesh):
    n_ctx, n_tp = mesh.devices.shape
    n_core = 2
    n_x = 4
    n_zl = n_tp // (n_core * n_x)
    fine = Mesh(mesh.devices.reshape(n_ctx, n_zl, n_x, n_core), ("ctx",) + TP_AXES)
    return jax.shard_map(
        layer,
        mesh=fine,
        in_specs=(
            P("ctx", None),
            P(),
            P(None, TP_AXES),
            P(None, TP_AXES),
            P(),
            P(),
            P(TP_AXES, None),
            P(TP_AXES),
        ),
        out_specs=P("ctx", TP_AXES),
        check_vma=False,
    )
```

profile of v0, /device:TPU:33, one launch (start us, length us, event | category | flops | bytes accessed | tf_op | source)
XLA Modules:
  0.0 133.4 jit_solution(10751163944317554307)
XLA Ops:
  0.0 2.6 %copy.26 = bf16[128,5376]{0,1:T(8,128)(2,1)} copy(bf16[128,5376]{1,0:T(8,128)(2,1)} %param.14) | data formatting | bytes 2752512 | tf_op args[6]
  2.6 8.7 %all-to-all-start = ((bf16[128,24,224]{0,2,1:T(8,128)(2,1)}), bf16[128,24,224]{0,2,1:T(8,128)(2,1)S(1)}, u32[]{:S(2)}, u32[]{:S(2)}) async-start(bf16[128,24,224]{0,2,1:T(8,128)(2,1)} %bitcast.32), calls=%async_computation | async-start | bytes 2752512 | tf_op jit(solution)/shard_map/all_to_all | solution.py:71
  11.3 3.7 %fusion = f32[512]{0:T(512)S(1)} fusion(bf16[512,5376]{1,0:T(8,128)(2,1)} %param.8), kind=kLoop, calls=%fused_computation.2 | loop fusion | flops 8257024 | bytes 5507072 | tf_op jit(solution)/shard_map/reduce_sum | solution.py:42
  15.1 4.6 %multiply_reduce_fusion.1 = (f32[512]{0:T(512)S(1)}, f32[512,128]{0,1:T(8,128)S(1)}) fusion(bf16[5376,128]{1,0:T(8,128)(2,1)S(1)} %copy-done, bf16[512,5376]{1,0:T(8,128)(2,1)} %param.8, f32[5376]{0:T(1024)S(1)} %copy-done.4, f32[512]{0:T(512)S(1)} %add_rsqrt_fusion.3), kind=kOutput, calls=%fused_computation.47 | convolution fusion | flops 715783680 | bytes 7169024 | tf_op jit(solution)/shard_map/dot_general | solution.py:67
  19.7 0.5 multiply_sine_fusion
  20.4 0.1 fusion.28
  20.5 12.5 %collective-permute-start = (bf16[512,128]{0,1:T(8,128)(2,1)S(1)}, bf16[512,128]{0,1:T(8,128)(2,1)}, u32[]{:S(2)}, u32[]{:S(2)}) collective-permute-start(bf16[512,128]{0,1:T(8,128)(2,1)S(1)} %fusion.28), channel_id=1, source_target_pairs={{0,72},{24,0},{48,24},{72,48},{96,168},{120,96},{144,120},{168,144... | collective-permute-start | bytes 393224 | tf_op jit(solution)/shard_map/ppermute | solution.py:80
  33.0 1.9 %collective-permute-start.2 = (bf16[512,128]{0,1:T(8,128)(2,1)S(1)}, bf16[512,128]{0,1:T(8,128)(2,1)S(1)}, u32[]{:S(2)}, u32[]{:S(2)}) collective-permute-start(bf16[512,128]{0,1:T(8,128)(2,1)S(1)} %fusion.28), channel_id=1, source_target_pairs={{0,24},{24,48},{48,72},{72,96},{96,120},{120,144},{144,168},{168,1... | collective-permute-start | bytes 393224 | tf_op jit(solution)/shard_map/ppermute | solution.py:20
  35.0 5.0 %multiply_reduce_fusion.2 = (f32[512]{0:T(512)S(1)}, f32[512,128]{0,1:T(8,128)S(1)}) fusion(bf16[5376,128]{1,0:T(8,128)(2,1)} %param.10, bf16[512,5376]{1,0:T(8,128)(2,1)} %param.8, f32[5376]{0:T(1024)S(1)} %copy-done.4, f32[512]{0:T(512)S(1)} %add_rsqrt_fusion.3), kind=kOutput, calls=%fused_computation.49 | convolution fusion | flops 715783680 | bytes 7169024 | tf_op jit(solution)/shard_map/dot_general | solution.py:92
  40.0 6.5 %collective-permute-start.1 = (bf16[512,128]{0,1:T(8,128)(2,1)}, bf16[512,128]{0,1:T(8,128)(2,1)S(1)}, u32[]{:S(2)}, u32[]{:S(2)}) collective-permute-start(bf16[512,128]{0,1:T(8,128)(2,1)} %collective-permute-done), channel_id=1, source_target_pairs={{72,48},{0,72},{24,96},{48,120},{168,144},{96,168},{120,192},{144,... | collective-permute-start | bytes 393224 | tf_op jit(solution)/shard_map/ppermute | solution.py:80
  46.6 4.5 %collective-permute-done.2 = bf16[512,128]{0,1:T(8,128)(2,1)S(1)} collective-permute-done((bf16[512,128]{0,1:T(8,128)(2,1)S(1)}, bf16[512,128]{0,1:T(8,128)(2,1)S(1)}, u32[]{:S(2)}, u32[]{:S(2)}) %collective-permute-start.2) | collective-permute-done | bytes 131104 | tf_op jit(solution)/shard_map/ppermute | solution.py:20
  51.1 1.6 %collective-permute-done.1 = bf16[512,128]{0,1:T(8,128)(2,1)S(1)} collective-permute-done((bf16[512,128]{0,1:T(8,128)(2,1)}, bf16[512,128]{0,1:T(8,128)(2,1)S(1)}, u32[]{:S(2)}, u32[]{:S(2)}) %collective-permute-start.1) | collective-permute-done | bytes 131104 | tf_op jit(solution)/shard_map/ppermute | solution.py:80
  52.7 0.8 pad_maximum_fusion
  53.5 3.9 %collective-permute-start.3 = (bf16[1536,128]{0,1:T(8,128)(2,1)}, bf16[1536,128]{0,1:T(8,128)(2,1)}, u32[]{:S(2)}, u32[]{:S(2)}) collective-permute-start(bf16[1536,128]{0,1:T(8,128)(2,1)} %pad_maximum_fusion), channel_id=1, source_target_pairs={{0,1},{1,0},{2,3},{3,2},{4,5},{5,4},{6,7},{7,6},{8,9},{9,8},{10,11... | collective-permute-start | bytes 1179656 | tf_op jit(solution)/shard_map/ppermute | solution.py:85
  57.5 0.5 copy.27
  58.0 1.3 copy.45
  59.3 2.4 %fusion.35 = (f32[512]{0:T(512)S(1)}, f32[512,1536]{1,0:T(8,128)S(1)}) fusion(bf16[1536,128]{0,1:T(8,128)(2,1)} %pad_maximum_fusion, bf16[1536,128]{0,1:T(8,128)(2,1)} %collective-permute-done.3, pred[]{:T(512)S(6)} %eq.3, f32[512,128]{0,1:T(8,128)S(1)} %multiply_multiply_fusion.1, f32[512,64]{0,1:T(8,128)S(1)} %get-tuple-element.18, ...), kind=kOutput, calls=%fused_computation.67 | convolution fusion | flops 207552000 | bytes 4730369 | tf_op jit(solution)/shard_map/dot_general | solution.py:100
  61.7 0.6 fusion.5
  62.3 1.7 %fusion.12 = bf16[512,128]{1,0:T(8,128)(2,1)S(1)} fusion(f32[512,1536]{1,0:T(8,128)S(1)} %get-tuple-element.24, f32[512]{0:T(512)S(1)} %fusion.5, f32[512]{0:T(512)S(1)} %get-tuple-element.23, bf16[1536,128]{0,1:T(8,128)(2,1)} %collective-permute-done.3, bf16[1536,128]{0,1:T(8,128)(2,1)} %pad_maximum_fusion, pred[]{:T(512)S(6)} %eq.3), kind=kOutput, calls=%fused_computation.22 | convolution fusion | flops 203948032 | bytes 4067329 | tf_op jit(solution)/shard_map/dot_general | solution.py:110
  64.0 0.3 broadcast_in_dim.8
  64.3 40.8 %all_to_all.26 = bf16[12,512,128]{2,1,0:T(8,128)(2,1)} all-to-all(bf16[12,512,128]{2,1,0:T(8,128)(2,1)S(1)} %broadcast_in_dim.8), channel_id=1, replica_groups=mesh['ctx'=32,'zl'=3,'x'=4,'core'=2] {'zl','x'}, dimensions={0} | all-to-all | bytes 3145728 | tf_op jit(solution)/shard_map/all_to_all | solution.py:116
  105.1 4.2 %collective-permute-start.4 = (bf16[12,512,128]{2,1,0:T(8,128)(2,1)}, bf16[12,512,128]{2,1,0:T(8,128)(2,1)}, u32[]{:S(2)}, u32[]{:S(2)}) collective-permute-start(bf16[12,512,128]{2,1,0:T(8,128)(2,1)} %all_to_all.26), channel_id=1, source_target_pairs={{0,1},{1,0},{2,3},{3,2},{4,5},{5,4},{6,7},{7,6},{8,9},{9,8},{10,11... | collective-permute-start | bytes 4718600 | tf_op jit(solution)/shard_map/ppermute | solution.py:117
  109.3 3.7 %reshape.82 = bf16[12,2,128,224]{2,1,0,3:T(2,128)(2,1)S(1)} reshape(bf16[3072,224]{0,1:T(8,128)(2,1)} %bitcast.33) | data formatting | bytes 2752512 | tf_op jit(solution)/shard_map/reshape | solution.py:118
  113.0 3.3 %broadcast_select_fusion = (bf16[12,1,128,224]{2,1,0,3:T(2,128)(2,1)S(1)}, bf16[12,1,128,224]{2,1,0,3:T(2,128)(2,1)S(1)}) fusion(pred[]{:T(512)S(6)} %eq.3, bf16[12,2,128,224]{2,1,0,3:T(2,128)(2,1)S(1)} %reshape.82), kind=kLoop, calls=%fused_computation.13 | loop fusion | flops 688128 | bytes 2752513 | tf_op jit(solution)/shard_map/jit(_where)/select_n | solution.py:120
  116.3 2.1 %convolution_bitcast_fusion.1 = f32[512,224]{0,1:T(8,128)S(1)} fusion(bf16[12,512,128]{2,1,0:T(8,128)(2,1)} %all_to_all.26, bf16[12,1,128,224]{2,1,0,3:T(2,128)(2,1)S(1)} %get-tuple-element.12), kind=kOutput, calls=%fused_computation.20 | convolution fusion | flops 352321536 | bytes 2719744 | tf_op jit(solution)/shard_map/dot_general | solution.py:122
  118.4 2.1 %multiply_reduce_fusion = (f32[512]{0:T(512)S(1)}, f32[512,224]{0,1:T(8,128)S(1)}) fusion(f32[512,224]{0,1:T(8,128)S(1)} %convolution_bitcast_fusion.1, bf16[12,512,128]{2,1,0:T(8,128)(2,1)} %collective-permute-done.4, bf16[12,1,128,224]{2,1,0,3:T(2,128)(2,1)S(1)} %get-tuple-element.11), kind=kOutput, calls=%fused_computation.28 | convolution fusion | flops 352665088 | bytes 3180544 | tf_op jit(solution)/shard_map/dot_general | solution.py:124
  120.4 0.7 broadcast_in_dim.9
  121.1 4.6 %all-to-all-start.2 = ((f32[24,1,512]{2,1,0:T(1,128)}), f32[24,1,512]{2,1,0:T(1,128)S(1)}, u32[]{:S(2)}, u32[]{:S(2)}) async-start(f32[24,1,512]{2,1,0:T(1,128)} %broadcast_in_dim.9), calls=%async_computation.2 | async-start | bytes 98304 | tf_op jit(solution)/shard_map/all_to_all | solution.py:127
  125.7 1.1 constant_dynamic-slice_fusion
  126.9 0.1 copy.32
  127.0 5.5 %all-to-all-done.2 = f32[24,1,512]{2,1,0:T(1,128)S(1)} async-done(((f32[24,1,512]{2,1,0:T(1,128)}), f32[24,1,512]{2,1,0:T(1,128)S(1)}, u32[]{:S(2)}, u32[]{:S(2)}) %all-to-all-start.2) | async-done | bytes 49184 | tf_op jit(solution)/shard_map/all_to_all | solution.py:127
  132.6 0.8 add_convert_fusion
  (27 shorter events, 0.4 us)
Async XLA Ops:
  0.0 15.1 %copy-start = (bf16[5376,128]{1,0:T(8,128)(2,1)S(1)}, bf16[5376,128]{1,0:T(8,128)(2,1)}, u32[]{:S(2)}) copy-start(bf16[5376,128]{1,0:T(8,128)(2,1)} %param.11) | copy-start | bytes 4128772
  2.6 54.9 %all-to-all-start = ((bf16[128,24,224]{0,2,1:T(8,128)(2,1)}), bf16[128,24,224]{0,2,1:T(8,128)(2,1)S(1)}, u32[]{:S(2)}, u32[]{:S(2)}) async-start(bf16[128,24,224]{0,2,1:T(8,128)(2,1)} %bitcast.32), calls=%async_computation | async-start | bytes 2752512 | tf_op jit(solution)/shard_map/all_to_all | solution.py:71
  11.3 3.8 %copy-start.4 = (f32[5376]{0:T(1024)S(1)}, f32[5376]{0:T(1024)}, u32[]{:S(2)}) copy-start(f32[5376]{0:T(1024)} %param.9) | copy-start | bytes 64516
  15.1 5.2 %copy-start.1 = (f32[128]{0:T(128)S(1)}, f32[128]{0:T(128)}, u32[]{:S(2)}) copy-start(f32[128]{0:T(128)} %param.13) | copy-start | bytes 1540
  20.5 19.5 %collective-permute-start = (bf16[512,128]{0,1:T(8,128)(2,1)S(1)}, bf16[512,128]{0,1:T(8,128)(2,1)}, u32[]{:S(2)}, u32[]{:S(2)}) collective-permute-start(bf16[512,128]{0,1:T(8,128)(2,1)S(1)} %fusion.28), channel_id=1, source_target_pairs={{0,72},{24,0},{48,24},{72,48},{96,168},{120,96},{144,120},{168,144... | collective-permute-start | bytes 393224 | tf_op jit(solution)/shard_map/ppermute | solution.py:80
  33.0 18.1 %collective-permute-start.2 = (bf16[512,128]{0,1:T(8,128)(2,1)S(1)}, bf16[512,128]{0,1:T(8,128)(2,1)S(1)}, u32[]{:S(2)}, u32[]{:S(2)}) collective-permute-start(bf16[512,128]{0,1:T(8,128)(2,1)S(1)} %fusion.28), channel_id=1, source_target_pairs={{0,24},{24,48},{48,72},{72,96},{96,120},{120,144},{144,168},{168,1... | collective-permute-start | bytes 393224 | tf_op jit(solution)/shard_map/ppermute | solution.py:20
  35.0 11.6 %copy-start.3 = (f32[128]{0:T(128)S(1)}, f32[128]{0:T(128)}, u32[]{:S(2)}) copy-start(f32[128]{0:T(128)} %param.12) | copy-start | bytes 1540
  40.0 12.7 %collective-permute-start.1 = (bf16[512,128]{0,1:T(8,128)(2,1)}, bf16[512,128]{0,1:T(8,128)(2,1)S(1)}, u32[]{:S(2)}, u32[]{:S(2)}) collective-permute-start(bf16[512,128]{0,1:T(8,128)(2,1)} %collective-permute-done), channel_id=1, source_target_pairs={{72,48},{0,72},{24,96},{48,120},{168,144},{96,168},{120,192},{144,... | collective-permute-start | bytes 393224 | tf_op jit(solution)/shard_map/ppermute | solution.py:80
  53.5 5.9 %collective-permute-start.3 = (bf16[1536,128]{0,1:T(8,128)(2,1)}, bf16[1536,128]{0,1:T(8,128)(2,1)}, u32[]{:S(2)}, u32[]{:S(2)}) collective-permute-start(bf16[1536,128]{0,1:T(8,128)(2,1)} %pad_maximum_fusion), channel_id=1, source_target_pairs={{0,1},{1,0},{2,3},{3,2},{4,5},{5,4},{6,7},{7,6},{8,9},{9,8},{10,11... | collective-permute-start | bytes 1179656 | tf_op jit(solution)/shard_map/ppermute | solution.py:85
  105.1 13.3 %collective-permute-start.4 = (bf16[12,512,128]{2,1,0:T(8,128)(2,1)}, bf16[12,512,128]{2,1,0:T(8,128)(2,1)}, u32[]{:S(2)}, u32[]{:S(2)}) collective-permute-start(bf16[12,512,128]{2,1,0:T(8,128)(2,1)} %all_to_all.26), channel_id=1, source_target_pairs={{0,1},{1,0},{2,3},{3,2},{4,5},{5,4},{6,7},{7,6},{8,9},{9,8},{10,11... | collective-permute-start | bytes 4718600 | tf_op jit(solution)/shard_map/ppermute | solution.py:117
  116.3 16.3 %copy-start.2 = (f32[224]{0:T(256)S(1)}, f32[224]{0:T(256)}, u32[]{:S(2)}) copy-start(f32[224]{0:T(256)} %param.15) | copy-start | bytes 2692
  121.1 11.5 %all-to-all-start.2 = ((f32[24,1,512]{2,1,0:T(1,128)}), f32[24,1,512]{2,1,0:T(1,128)S(1)}, u32[]{:S(2)}, u32[]{:S(2)}) async-start(f32[24,1,512]{2,1,0:T(1,128)} %broadcast_in_dim.9), calls=%async_computation.2 | async-start | bytes 98304 | tf_op jit(solution)/shard_map/all_to_all | solution.py:127
where the time goes:
time: 134 us; the launch traced here: 133 us
  starting transfers between devices  42.3 us (32%)
  blocking collectives  40.8 us (30%)
  matrix products  17.9 us (13%)
  waiting for transfers between devices  11.6 us (9%)
  local copies, waits for them, and re-layouts  10.4 us (8%)
  other arithmetic  10.1 us (8%)
    all_to_all x1, blocking collectives, layer(): own_heads = lax.all_to_all(copies, ('zl', 'x'), 0, 0, tiled=True)  40.8 us
    ppermute x1, starting transfers between devices, layer(): lax.ppermute(own_block, 'ctx', first_leg)  12.5 us
    all_to_all x1, starting transfers between devices, layer(): lax.all_to_all(out_weight.reshape(head_width, n_tp, col_share), TP_AXES,...  8.66 us
    ppermute x1, starting transfers between devices, layer(): lax.ppermute(lax.ppermute(own_block, 'ctx', first_leg), 'ctx', second_leg)  6.48 us
    all_to_all x1, waiting for transfers between devices, layer(): lax.all_to_all(square_copies, TP_AXES, 0, 0, tiled=True)  5.54 us
    dot_general x1, matrix products, layer(): queries = jnp.dot(normed, query_weight, preferred_element_type=jnp.float32)  5.03 us
    dot_general x1, matrix products, layer(): jnp.dot(normed, keyval_weight, preferred_element_type=jnp.float32)  4.63 us
    all_to_all x1, starting transfers between devices, layer(): lax.all_to_all(square_copies, TP_AXES, 0, 0, tiled=True)  4.61 us
  transfers between devices with their start and end apart: 7, of which 3 were waited for; matrix products, arithmetic and copies ran while one was open for 20% of the time, Pallas kernels for 0%

commit v1 on v0

--- a/solution.py
+++ b/solution.py
@@ -1,6 +1,7 @@
 import jax
 import jax.numpy as jnp
 from jax import lax
+from jax.experimental import pallas as pl
 from jax.sharding import Mesh, PartitionSpec as P
 
 WIN = 1024
@@ -11,7 +12,6 @@
 rope_base = 10000.0
 
 TP_AXES = ("zl", "x", "core")
-Z_HI = 4
 
 
 def from_behind(block, axis, distance):
@@ -44,6 +44,36 @@
     )
 
 
+def norm_project_kernel(rows_ref, gain_ref, weight_ref, projected_ref, normed_ref):
+    rows = rows_ref[...].astype(jnp.float32)
+    scale = lax.rsqrt(jnp.mean(rows * rows, axis=-1, keepdims=True) + epsilon)
+    normed = (rows * scale * gain_ref[...]).astype(jnp.bfloat16)
+    normed_ref[...] = normed
+    projected_ref[...] = jnp.dot(normed, weight_ref[...], preferred_element_type=jnp.float32)
+
+
+def norm_project(tokens, norm_gain, weight, block_rows=128):
+    tok_rows, model_width = tokens.shape
+    width = weight.shape[1]
+    return pl.pallas_call(
+        norm_project_kernel,
+        grid=(tok_rows // block_rows,),
+        in_specs=[
+            pl.BlockSpec((block_rows, model_width), lambda i: (i, 0)),
+            pl.BlockSpec((1, model_width), lambda i: (0, 0)),
+            pl.BlockSpec((model_width, width), lambda i: (0, 0)),
+        ],
+        out_specs=[
+            pl.BlockSpec((block_rows, width), lambda i: (i, 0)),
+            pl.BlockSpec((block_rows, model_width), lambda i: (i, 0)),
+        ],
+        out_shape=[
+            jax.ShapeDtypeStruct((tok_rows, width), jnp.float32),
+            jax.ShapeDtypeStruct((tok_rows, model_width), jnp.bfloat16),
+        ],
+    )(tokens, norm_gain.reshape(1, model_width), weight)
+
+
 def layer(
     tokens, norm_gain, query_weight, keyval_weight, query_gain, key_gain, out_weight, post_gain
 ):
@@ -59,12 +89,10 @@
     tp_index = (lax.axis_index("zl") * n_x + lax.axis_index("x")) * n_core + core_index
     is_even = core_index == 0
 
-    as_float = tokens.astype(jnp.float32)
-    normed = rms_scale(as_float, norm_gain).astype(jnp.bfloat16)
     positions = ctx_index * tok_rows + jnp.arange(tok_rows, dtype=jnp.int32)
     cosine, sine_table = rope_tables(positions, head_width)
 
-    projected = jnp.dot(normed, keyval_weight, preferred_element_type=jnp.float32)
+    projected, normed = norm_project(tokens, norm_gain, keyval_weight)
     rotated = rotate(rms_scale(projected, key_gain), cosine, sine_table)
     own_block = jnp.where(is_even, rotated, projected).astype(jnp.bfloat16)
     n_tp = n_zl * n_x * n_core
@@ -72,15 +100,7 @@
         out_weight.reshape(head_width, n_tp, col_share), TP_AXES, 1, 0, tiled=True
     ).reshape(n_tp * head_width, col_share)
     span_count = WIN // tok_rows
-    n_ctx = lax.axis_size("ctx")
-    devices = range(n_ctx)
-    mid = [(c // Z_HI) * Z_HI + (c % Z_HI - 1) % Z_HI for c in devices]
-    first_leg = [(c, mid[c]) for c in devices if c + span_count in devices]
-    second_leg = [(mid[c], c + span_count) for c in devices if c + span_count in devices]
-    far_block = lax.ppermute(lax.ppermute(own_block, "ctx", first_leg), "ctx", second_leg)
-    earlier = [far_block] + [
-        from_behind(own_block, "ctx", offset) for offset in range(span_count - 1, 0, -1)
-    ]
+    earlier = [from_behind(own_block, "ctx", offset) for offset in range(span_count, 0, -1)]
     own_window = jnp.concatenate(earlier + [own_block], axis=0)
     other_window = lax.ppermute(own_window, "core", [(0, 1), (1, 0)])
     weight_block, own_window, other_window = lax.optimization_barrier(

time: 134 us -> 132 us (0.985)
  the two profiles are of different devices: /device:TPU:33 before, /device:TPU:56 now
where the time goes in v1:
time: 132 us; the launch traced here: 131 us
  starting transfers between devices  36.3 us (27%)
  blocking collectives  31.3 us (24%)
  waiting for transfers between devices  18.8 us (14%)
  other arithmetic  12.9 us (10%)
  matrix products  12.8 us (10%)
  local copies, waits for them, and re-layouts  11.8 us (9%)
  Pallas kernels  7.1 us (5%)
    all_to_all x1, blocking collectives, layer(): own_heads = lax.all_to_all(copies, ('zl', 'x'), 0, 0, tiled=True)  31.3 us
    ppermute x2, starting transfers between devices, from_behind(): return lax.ppermute(block, axis, route)  19.1 us
    ppermute x2, waiting for transfers between devices, from_behind(): return lax.ppermute(block, axis, route)  13 us
    all_to_all x1, starting transfers between devices, layer(): lax.all_to_all(out_weight.reshape(head_width, n_tp, col_share), TP_AXES,...  8.3 us
    pallas_call x1, Pallas kernels, norm_project(): pl.pallas_call(norm_project_kernel, grid=(tok_rows // block_rows,), in_sp...  7.1 us
    all_to_all x1, waiting for transfers between devices, layer(): lax.all_to_all(square_copies, TP_AXES, 0, 0, tiled=True)  5.75 us
    all_to_all x1, starting transfers between devices, layer(): lax.all_to_all(square_copies, TP_AXES, 0, 0, tiled=True)  4.86 us
    dot_general x1, matrix products, layer(): queries = jnp.dot(normed, query_weight, preferred_element_type=jnp.float32)  4.52 us
  transfers between devices with their start and end apart: 6, of which 3 were waited for; matrix products, arithmetic and copies ran while one was open for 20% of the time, Pallas kernels for 5%

profile of v1, /device:TPU:56, one launch (start us, length us, event | category | flops | bytes accessed | tf_op | source)
XLA Modules:
  0.0 131.3 jit_solution(769987837264829693)
XLA Ops:
  0.0 2.6 %copy.31 = bf16[128,5376]{0,1:T(8,128)(2,1)} copy(bf16[128,5376]{1,0:T(8,128)(2,1)} %param.14) | data formatting | bytes 2752512 | tf_op args[6]
  2.6 8.3 %all-to-all-start = ((bf16[128,24,224]{0,2,1:T(8,128)(2,1)}), bf16[128,24,224]{0,2,1:T(8,128)(2,1)S(1)}, u32[]{:S(2)}, u32[]{:S(2)}) async-start(bf16[128,24,224]{0,2,1:T(8,128)(2,1)} %bitcast.32), calls=%async_computation | async-start | bytes 2752512 | tf_op jit(solution)/shard_map/all_to_all | solution.py:99
  10.9 0.6 reshape.74.gain_ref
  11.6 7.1 %shard_map.82 = (f32[512,128]{1,0:T(8,128)}, bf16[512,5376]{1,0:T(8,128)(2,1)}) custom-call(bf16[512,5376]{1,0:T(8,128)(2,1)} %rows_ref.1, f32[1,5376]{1,0:T(1,128)} %reshape.74.gain_ref, bf16[5376,128]{1,0:T(8,128)(2,1)} %weight_ref.1), custom_call_target="tpu_custom_call" | custom-call | tf_op jit(solution)/shard_map/pallas_call | solution.py:58
  18.7 1.1 multiply_reduce_fusion.1
  19.9 1.0 multiply_cosine_fusion
  20.9 1.1 multiply_multiply_fusion
  22.1 1.0 fusion.19
  23.1 9.1 %collective-permute-start.1 = (bf16[512,128]{1,0:T(8,128)(2,1)}, bf16[512,128]{1,0:T(8,128)(2,1)}, u32[]{:S(2)}, u32[]{:S(2)}) collective-permute-start(bf16[512,128]{1,0:T(8,128)(2,1)} %fusion.19), channel_id=1, source_target_pairs={{0,24},{24,48},{48,72},{72,96},{96,120},{120,144},{144,168},{168,1... | collective-permute-start | bytes 393224 | tf_op jit(solution)/shard_map/ppermute | solution.py:20
  32.2 10.0 %collective-permute-start = (bf16[512,128]{1,0:T(8,128)(2,1)}, bf16[512,128]{1,0:T(8,128)(2,1)}, u32[]{:S(2)}, u32[]{:S(2)}) collective-permute-start(bf16[512,128]{1,0:T(8,128)(2,1)} %fusion.19), channel_id=1, source_target_pairs={{0,48},{24,72},{48,96},{72,120},{96,144},{120,168},{144,192},{168,... | collective-permute-start | bytes 393224 | tf_op jit(solution)/shard_map/ppermute | solution.py:20
  42.3 4.5 %multiply_reduce_fusion.2 = (f32[512]{0:T(512)S(1)}, f32[512,128]{0,1:T(8,128)S(1)}) fusion(bf16[512,5376]{1,0:T(8,128)(2,1)} %get-tuple-element.10, bf16[5376,128]{1,0:T(8,128)(2,1)S(1)} %copy-done), kind=kOutput, calls=%fused_computation.44 | convolution fusion | flops 704773632 | bytes 7145472 | tf_op jit(solution)/shard_map/dot_general | solution.py:112
  46.8 0.8 copy.30
  47.6 1.1 multiply_multiply_fusion.1
  48.7 6.4 %collective-permute-done.1 = bf16[512,128]{1,0:T(8,128)(2,1)} collective-permute-done((bf16[512,128]{1,0:T(8,128)(2,1)}, bf16[512,128]{1,0:T(8,128)(2,1)}, u32[]{:S(2)}, u32[]{:S(2)}) %collective-permute-start.1) | collective-permute-done | bytes 131104 | tf_op jit(solution)/shard_map/ppermute | solution.py:20
  55.1 6.7 %collective-permute-done = bf16[512,128]{1,0:T(8,128)(2,1)} collective-permute-done((bf16[512,128]{1,0:T(8,128)(2,1)}, bf16[512,128]{1,0:T(8,128)(2,1)}, u32[]{:S(2)}, u32[]{:S(2)}) %collective-permute-start) | collective-permute-done | bytes 131104 | tf_op jit(solution)/shard_map/ppermute | solution.py:20
  61.8 1.8 %pad_maximum_fusion = bf16[1536,128]{1,0:T(8,128)(2,1)} fusion(bf16[512,128]{1,0:T(8,128)(2,1)} %fusion.19, bf16[512,128]{1,0:T(8,128)(2,1)} %collective-permute-done.1, bf16[512,128]{1,0:T(8,128)(2,1)} %collective-permute-done), kind=kLoop, calls=%fused_computation.22 | loop fusion | flops 1179648 | bytes 786432 | tf_op jit(solution)/shard_map/concatenate | solution.py:104
  63.6 1.9 %collective-permute-start.2 = (bf16[1536,128]{1,0:T(8,128)(2,1)}, bf16[1536,128]{1,0:T(8,128)(2,1)}, u32[]{:S(2)}, u32[]{:S(2)}) collective-permute-start(bf16[1536,128]{1,0:T(8,128)(2,1)} %pad_maximum_fusion), channel_id=1, source_target_pairs={{0,1},{1,0},{2,3},{3,2},{4,5},{5,4},{6,7},{7,6},{8,9},{9,8},{10,11... | collective-permute-start | bytes 1179656 | tf_op jit(solution)/shard_map/ppermute | solution.py:105
  65.5 0.9 slice_negate_fusion.1
  67.0 1.3 copy.50
  68.3 2.5 %fusion.25 = (f32[512]{0:T(512)S(1)}, f32[512,1536]{1,0:T(8,128)S(1)}) fusion(bf16[1536,128]{1,0:T(8,128)(2,1)} %pad_maximum_fusion, bf16[1536,128]{1,0:T(8,128)(2,1)} %collective-permute-done.2, pred[]{:T(512)S(6)} %eq.3, f32[512,64]{1,0:T(8,128)S(1)} %copy-done.3, f32[512,64]{1,0:T(8,128)S(1)} %copy-done.2, f32[512,128]{1,0:T(8,128)S(1)} %multiply_multiply_fusion.1, ...), kind=kOutput, calls=%fused_computation.57 | convolution fusion | flops 207552000 | bytes 4730369 | tf_op jit(solution)/shard_map/dot_general | solution.py:120
  71.3 1.7 %fusion.5 = bf16[512,128]{1,0:T(8,128)(2,1)S(1)} fusion(f32[512,1536]{1,0:T(8,128)S(1)} %get-tuple-element.26, f32[512]{0:T(512)S(1)} %fusion.2, f32[512]{0:T(512)S(1)} %get-tuple-element.25, bf16[1536,128]{1,0:T(8,128)(2,1)} %collective-permute-done.2, bf16[1536,128]{1,0:T(8,128)(2,1)} %pad_maximum_fusion, pred[]{:T(512)S(6)} %eq.3), kind=kOutput, calls=%fused_computation.15 | convolution fusion | flops 203948032 | bytes 4067329 | tf_op jit(solution)/shard_map/dot_general | solution.py:130
  73.3 31.3 %all_to_all.26 = bf16[12,512,128]{2,1,0:T(8,128)(2,1)} all-to-all(bf16[12,512,128]{2,1,0:T(8,128)(2,1)S(1)} %broadcast_in_dim.8), channel_id=1, replica_groups=mesh['ctx'=32,'zl'=3,'x'=4,'core'=2] {'zl','x'}, dimensions={0} | all-to-all | bytes 3145728 | tf_op jit(solution)/shard_map/all_to_all | solution.py:136
  104.6 2.1 %collective-permute-start.3 = (bf16[12,512,128]{2,1,0:T(8,128)(2,1)}, bf16[12,512,128]{2,1,0:T(8,128)(2,1)}, u32[]{:S(2)}, u32[]{:S(2)}) collective-permute-start(bf16[12,512,128]{2,1,0:T(8,128)(2,1)} %all_to_all.26), channel_id=1, source_target_pairs={{0,1},{1,0},{2,3},{3,2},{4,5},{5,4},{6,7},{7,6},{8,9},{9,8},{10,11... | collective-permute-start | bytes 4718600 | tf_op jit(solution)/shard_map/ppermute | solution.py:137
  106.7 3.7 %reshape.77 = bf16[12,2,128,224]{2,1,0,3:T(2,128)(2,1)S(1)} reshape(bf16[3072,224]{0,1:T(8,128)(2,1)} %bitcast.33) | data formatting | bytes 2752512 | tf_op jit(solution)/shard_map/reshape | solution.py:138
  110.4 3.3 %broadcast_select_fusion = (bf16[12,1,128,224]{2,1,0,3:T(2,128)(2,1)S(1)}, bf16[12,1,128,224]{2,1,0,3:T(2,128)(2,1)S(1)}) fusion(pred[]{:T(512)S(6)} %eq.3, bf16[12,2,128,224]{2,1,0,3:T(2,128)(2,1)S(1)} %reshape.77), kind=kLoop, calls=%fused_computation.8 | loop fusion | flops 688128 | bytes 2752513 | tf_op jit(solution)/shard_map/jit(_where)/select_n | solution.py:140
  113.7 2.0 %convolution_bitcast_fusion.1 = f32[512,224]{0,1:T(8,128)S(1)} fusion(bf16[12,512,128]{2,1,0:T(8,128)(2,1)} %all_to_all.26, bf16[12,1,128,224]{2,1,0,3:T(2,128)(2,1)S(1)} %get-tuple-element.16), kind=kOutput, calls=%fused_computation.13 | convolution fusion | flops 352321536 | bytes 2719744 | tf_op jit(solution)/shard_map/dot_general | solution.py:142
  115.7 2.1 %multiply_reduce_fusion = (f32[512]{0:T(512)S(1)}, f32[512,224]{0,1:T(8,128)S(1)}) fusion(f32[512,224]{0,1:T(8,128)S(1)} %convolution_bitcast_fusion.1, bf16[12,512,128]{2,1,0:T(8,128)(2,1)} %collective-permute-done.3, bf16[12,1,128,224]{2,1,0,3:T(2,128)(2,1)S(1)} %get-tuple-element.15), kind=kOutput, calls=%fused_computation.21 | convolution fusion | flops 352665088 | bytes 3180544 | tf_op jit(solution)/shard_map/dot_general | solution.py:144
  117.8 0.7 broadcast_in_dim.9
  118.5 4.9 %all-to-all-start.2 = ((f32[24,1,512]{2,1,0:T(1,128)}), f32[24,1,512]{2,1,0:T(1,128)S(1)}, u32[]{:S(2)}, u32[]{:S(2)}) async-start(f32[24,1,512]{2,1,0:T(1,128)} %broadcast_in_dim.9), calls=%async_computation.2 | async-start | bytes 98304 | tf_op jit(solution)/shard_map/all_to_all | solution.py:147
  123.3 1.1 constant_dynamic-slice_fusion
  124.6 5.8 %all-to-all-done.2 = f32[24,1,512]{2,1,0:T(1,128)S(1)} async-done(((f32[24,1,512]{2,1,0:T(1,128)}), f32[24,1,512]{2,1,0:T(1,128)S(1)}, u32[]{:S(2)}, u32[]{:S(2)}) %all-to-all-start.2) | async-done | bytes 49184 | tf_op jit(solution)/shard_map/all_to_all | solution.py:147
  130.5 0.8 add_convert_fusion
  (32 shorter events, 1.8 us)
Async XLA Ops:
  0.0 42.3 %copy-start = (bf16[5376,128]{1,0:T(8,128)(2,1)S(1)}, bf16[5376,128]{1,0:T(8,128)(2,1)}, u32[]{:S(2)}) copy-start(bf16[5376,128]{1,0:T(8,128)(2,1)} %param.10) | copy-start | bytes 4128772
  2.6 8.3 %copy-start.4 = (f32[5376]{0:T(1024)S(1)}, f32[5376]{0:T(1024)}, u32[]{:S(2)}) copy-start(f32[5376]{0:T(1024)} %param.9) | copy-start | bytes 64516
  2.6 63.8 %all-to-all-start = ((bf16[128,24,224]{0,2,1:T(8,128)(2,1)}), bf16[128,24,224]{0,2,1:T(8,128)(2,1)S(1)}, u32[]{:S(2)}, u32[]{:S(2)}) async-start(bf16[128,24,224]{0,2,1:T(8,128)(2,1)} %bitcast.32), calls=%async_computation | async-start | bytes 2752512 | tf_op jit(solution)/shard_map/all_to_all | solution.py:99
  11.6 9.3 %copy-start.5 = (f32[128]{0:T(128)S(1)}, f32[128]{0:T(128)}, u32[]{:S(2)}) copy-start(f32[128]{0:T(128)} %param.13) | copy-start | bytes 1540
  18.7 3.4 %copy-start.1 = (f32[512,128]{1,0:T(8,128)S(1)}, f32[512,128]{1,0:T(8,128)}, u32[]{:S(2)}) copy-start(f32[512,128]{1,0:T(8,128)} %get-tuple-element.11) | copy-start | bytes 786436
  23.1 32.0 %collective-permute-start.1 = (bf16[512,128]{1,0:T(8,128)(2,1)}, bf16[512,128]{1,0:T(8,128)(2,1)}, u32[]{:S(2)}, u32[]{:S(2)}) collective-permute-start(bf16[512,128]{1,0:T(8,128)(2,1)} %fusion.19), channel_id=1, source_target_pairs={{0,24},{24,48},{48,72},{72,96},{96,120},{120,144},{144,168},{168,1... | collective-permute-start | bytes 393224 | tf_op jit(solution)/shard_map/ppermute | solution.py:20
  32.2 29.6 %collective-permute-start = (bf16[512,128]{1,0:T(8,128)(2,1)}, bf16[512,128]{1,0:T(8,128)(2,1)}, u32[]{:S(2)}, u32[]{:S(2)}) collective-permute-start(bf16[512,128]{1,0:T(8,128)(2,1)} %fusion.19), channel_id=1, source_target_pairs={{0,48},{24,72},{48,96},{72,120},{96,144},{120,168},{144,192},{168,... | collective-permute-start | bytes 393224 | tf_op jit(solution)/shard_map/ppermute | solution.py:20
  42.3 5.4 %copy-start.7 = (f32[128]{0:T(128)S(1)}, f32[128]{0:T(128)}, u32[]{:S(2)}) copy-start(f32[128]{0:T(128)} %param.12) | copy-start | bytes 1540
  63.6 4.7 %collective-permute-start.2 = (bf16[1536,128]{1,0:T(8,128)(2,1)}, bf16[1536,128]{1,0:T(8,128)(2,1)}, u32[]{:S(2)}, u32[]{:S(2)}) collective-permute-start(bf16[1536,128]{1,0:T(8,128)(2,1)} %pad_maximum_fusion), channel_id=1, source_target_pairs={{0,1},{1,0},{2,3},{3,2},{4,5},{5,4},{6,7},{7,6},{8,9},{9,8},{10,11... | collective-permute-start | bytes 1179656 | tf_op jit(solution)/shard_map/ppermute | solution.py:105
  66.9 1.3 %copy-start.2 = (f32[512,64]{1,0:T(8,128)S(1)}, f32[512,64]{1,0:T(8,128)}, u32[]{:S(2)}) copy-start(f32[512,64]{1,0:T(8,128)} %get-tuple-element.17) | copy-start | bytes 393220
  66.9 1.3 %copy-start.3 = (f32[512,64]{1,0:T(8,128)S(1)}, f32[512,64]{1,0:T(8,128)}, u32[]{:S(2)}) copy-start(f32[512,64]{1,0:T(8,128)} %get-tuple-element.18) | copy-start | bytes 393220
  104.6 11.1 %collective-permute-start.3 = (bf16[12,512,128]{2,1,0:T(8,128)(2,1)}, bf16[12,512,128]{2,1,0:T(8,128)(2,1)}, u32[]{:S(2)}, u32[]{:S(2)}) collective-permute-start(bf16[12,512,128]{2,1,0:T(8,128)(2,1)} %all_to_all.26), channel_id=1, source_target_pairs={{0,1},{1,0},{2,3},{3,2},{4,5},{5,4},{6,7},{7,6},{8,9},{9,8},{10,11... | collective-permute-start | bytes 4718600 | tf_op jit(solution)/shard_map/ppermute | solution.py:137
  115.7 14.7 %copy-start.6 = (f32[224]{0:T(256)S(1)}, f32[224]{0:T(256)}, u32[]{:S(2)}) copy-start(f32[224]{0:T(256)} %param.15) | copy-start | bytes 2692
  118.5 11.9 %all-to-all-start.2 = ((f32[24,1,512]{2,1,0:T(1,128)}), f32[24,1,512]{2,1,0:T(1,128)S(1)}, u32[]{:S(2)}, u32[]{:S(2)}) async-start(f32[24,1,512]{2,1,0:T(1,128)} %broadcast_in_dim.9), calls=%async_computation.2 | async-start | bytes 98304 | tf_op jit(solution)/shard_map/all_to_all | solution.py:147

commit v2 on v1

--- a/solution.py
+++ b/solution.py
@@ -44,11 +44,11 @@
     )
 
 
-def norm_project_kernel(rows_ref, gain_ref, weight_ref, projected_ref, normed_ref):
+def norm_project_kernel(rows_ref, gain_ref, weight_ref, projected_ref, scale_ref):
     rows = rows_ref[...].astype(jnp.float32)
     scale = lax.rsqrt(jnp.mean(rows * rows, axis=-1, keepdims=True) + epsilon)
+    scale_ref[...] = scale
     normed = (rows * scale * gain_ref[...]).astype(jnp.bfloat16)
-    normed_ref[...] = normed
     projected_ref[...] = jnp.dot(normed, weight_ref[...], preferred_element_type=jnp.float32)
 
 
@@ -65,11 +65,11 @@
         ],
         out_specs=[
             pl.BlockSpec((block_rows, width), lambda i: (i, 0)),
-            pl.BlockSpec((block_rows, model_width), lambda i: (i, 0)),
+            pl.BlockSpec((block_rows, 1), lambda i: (i, 0)),
         ],
         out_shape=[
             jax.ShapeDtypeStruct((tok_rows, width), jnp.float32),
-            jax.ShapeDtypeStruct((tok_rows, model_width), jnp.bfloat16),
+            jax.ShapeDtypeStruct((tok_rows, 1), jnp.float32),
         ],
     )(tokens, norm_gain.reshape(1, model_width), weight)
 
@@ -92,7 +92,7 @@
     positions = ctx_index * tok_rows + jnp.arange(tok_rows, dtype=jnp.int32)
     cosine, sine_table = rope_tables(positions, head_width)
 
-    projected, normed = norm_project(tokens, norm_gain, keyval_weight)
+    projected, row_scale = norm_project(tokens, norm_gain, keyval_weight)
     rotated = rotate(rms_scale(projected, key_gain), cosine, sine_table)
     own_block = jnp.where(is_even, rotated, projected).astype(jnp.bfloat16)
     n_tp = n_zl * n_x * n_core
@@ -109,6 +109,7 @@
     key_window = jnp.where(is_even, own_window, other_window)
     value_window = jnp.where(is_even, other_window, own_window)
 
+    normed = (tokens.astype(jnp.float32) * row_scale * norm_gain).astype(jnp.bfloat16)
     queries = jnp.dot(normed, query_weight, preferred_element_type=jnp.float32)
     queries = (
         rotate(rms_scale(queries, query_gain), cosine, sine_table) * query_scalar ** (-0.5)

time: 132 us -> 132 us (level)
  blocking collectives: 31.3 us -> 36.5 us
  waiting for transfers between devices: 18.8 us -> 14.1 us
    all_to_all x1, blocking collectives: 31.3 us -> 36.5 us  [layer(): own_heads = lax.all_to_all(copies, ('zl', 'x'), 0, 0, tiled=True)]
    ppermute x2, waiting for transfers between devices: 13 us -> 8.3 us  [from_behind(): return lax.ppermute(block, axis, route)]
    unnamed x19 -> x21, local copies, waits for them, and re-layouts: 4.09 us -> 4.1 us
where the time goes in v2:
time: 132 us; the launch traced here: 131 us
  blocking collectives  36.5 us (28%)
  starting transfers between devices  35.7 us (27%)
  waiting for transfers between devices  14.1 us (11%)
  other arithmetic  13 us (10%)
  matrix products  12.9 us (10%)
  local copies, waits for them, and re-layouts  11.8 us (9%)
  Pallas kernels  6.53 us (5%)
    all_to_all x1, blocking collectives, layer(): own_heads = lax.all_to_all(copies, ('zl', 'x'), 0, 0, tiled=True)  36.5 us
    ppermute x2, starting transfers between devices, from_behind(): return lax.ppermute(block, axis, route)  18.5 us
    ppermute x2, waiting for transfers between devices, from_behind(): return lax.ppermute(block, axis, route)  8.3 us
    all_to_all x1, starting transfers between devices, layer(): lax.all_to_all(out_weight.reshape(head_width, n_tp, col_share), TP_AXES,...  8.3 us
    pallas_call x1, Pallas kernels, norm_project(): pl.pallas_call(norm_project_kernel, grid=(tok_rows // block_rows,), in_sp...  6.53 us
    all_to_all x1, waiting for transfers between devices, layer(): lax.all_to_all(square_copies, TP_AXES, 0, 0, tiled=True)  5.75 us
    all_to_all x1, starting transfers between devices, layer(): lax.all_to_all(square_copies, TP_AXES, 0, 0, tiled=True)  4.86 us
    dot_general x1, matrix products, layer(): queries = jnp.dot(normed, query_weight, preferred_element_type=jnp.float32)  4.63 us
  transfers between devices with their start and end apart: 6, of which 3 were waited for; matrix products, arithmetic and copies ran while one was open for 20% of the time, Pallas kernels for 5%

profile of v2, /device:TPU:56, one launch (start us, length us, event | category | flops | bytes accessed | tf_op | source)
XLA Modules:
  0.0 130.8 jit_solution(15608350858484694940)
XLA Ops:
  0.0 2.6 %copy.31 = bf16[128,5376]{0,1:T(8,128)(2,1)} copy(bf16[128,5376]{1,0:T(8,128)(2,1)} %param.14) | data formatting | bytes 2752512 | tf_op args[6]
  2.6 8.3 %all-to-all-start = ((bf16[128,24,224]{0,2,1:T(8,128)(2,1)}), bf16[128,24,224]{0,2,1:T(8,128)(2,1)S(1)}, u32[]{:S(2)}, u32[]{:S(2)}) async-start(bf16[128,24,224]{0,2,1:T(8,128)(2,1)} %bitcast.31), calls=%async_computation | async-start | bytes 2752512 | tf_op jit(solution)/shard_map/all_to_all | solution.py:99
  10.9 0.6 reshape.75.gain_ref
  11.6 6.5 %shard_map.82 = (f32[512,128]{1,0:T(8,128)}, f32[512,1]{1,0:T(8,128)}) custom-call(bf16[512,5376]{1,0:T(8,128)(2,1)} %rows_ref.1, f32[1,5376]{1,0:T(1,128)} %reshape.75.gain_ref, bf16[5376,128]{1,0:T(8,128)(2,1)} %weight_ref.1), custom_call_target="tpu_custom_call" | custom-call | tf_op jit(solution)/shard_map/pallas_call | solution.py:58
  18.1 1.1 multiply_reduce_fusion.1
  19.3 1.1 multiply_multiply_fusion
  20.4 1.0 multiply_cosine_fusion
  21.5 1.0 fusion.22
  22.5 13.9 %collective-permute-start = (bf16[512,128]{1,0:T(8,128)(2,1)}, bf16[512,128]{1,0:T(8,128)(2,1)}, u32[]{:S(2)}, u32[]{:S(2)}) collective-permute-start(bf16[512,128]{1,0:T(8,128)(2,1)} %fusion.22), channel_id=1, source_target_pairs={{0,48},{24,72},{48,96},{72,120},{96,144},{120,168},{144,192},{168,... | collective-permute-start | bytes 393224 | tf_op jit(solution)/shard_map/ppermute | solution.py:20
  36.5 4.6 %collective-permute-start.1 = (bf16[512,128]{1,0:T(8,128)(2,1)}, bf16[512,128]{1,0:T(8,128)(2,1)}, u32[]{:S(2)}, u32[]{:S(2)}) collective-permute-start(bf16[512,128]{1,0:T(8,128)(2,1)} %fusion.22), channel_id=1, source_target_pairs={{0,24},{24,48},{48,72},{72,96},{96,120},{120,144},{144,168},{168,1... | collective-permute-start | bytes 393224 | tf_op jit(solution)/shard_map/ppermute | solution.py:20
  41.2 4.6 %multiply_reduce_fusion.2 = (f32[512]{0:T(512)S(1)}, f32[512,128]{0,1:T(8,128)S(1)}) fusion(bf16[5376,128]{1,0:T(8,128)(2,1)S(1)} %copy-done, bf16[512,5376]{1,0:T(8,128)(2,1)} %rows_ref.1, f32[5376]{0:T(1024)} %param.9, f32[512]{0:T(512)S(1)} %reduce.1), kind=kOutput, calls=%fused_computation.48 | convolution fusion | flops 715783680 | bytes 7169024 | tf_op jit(solution)/shard_map/dot_general | solution.py:113
  45.9 0.8 copy.30
  46.7 1.1 multiply_multiply_fusion.1
  47.8 4.1 %collective-permute-done = bf16[512,128]{1,0:T(8,128)(2,1)} collective-permute-done((bf16[512,128]{1,0:T(8,128)(2,1)}, bf16[512,128]{1,0:T(8,128)(2,1)}, u32[]{:S(2)}, u32[]{:S(2)}) %collective-permute-start) | collective-permute-done | bytes 131104 | tf_op jit(solution)/shard_map/ppermute | solution.py:20
  51.9 4.2 %collective-permute-done.1 = bf16[512,128]{1,0:T(8,128)(2,1)} collective-permute-done((bf16[512,128]{1,0:T(8,128)(2,1)}, bf16[512,128]{1,0:T(8,128)(2,1)}, u32[]{:S(2)}, u32[]{:S(2)}) %collective-permute-start.1) | collective-permute-done | bytes 131104 | tf_op jit(solution)/shard_map/ppermute | solution.py:20
  56.1 1.8 %pad_maximum_fusion = bf16[1536,128]{1,0:T(8,128)(2,1)} fusion(bf16[512,128]{1,0:T(8,128)(2,1)} %fusion.22, bf16[512,128]{1,0:T(8,128)(2,1)} %collective-permute-done.1, bf16[512,128]{1,0:T(8,128)(2,1)} %collective-permute-done), kind=kLoop, calls=%fused_computation.26 | loop fusion | flops 1179648 | bytes 786432 | tf_op jit(solution)/shard_map/concatenate | solution.py:104
  57.9 1.9 %collective-permute-start.2 = (bf16[1536,128]{1,0:T(8,128)(2,1)}, bf16[1536,128]{1,0:T(8,128)(2,1)}, u32[]{:S(2)}, u32[]{:S(2)}) collective-permute-start(bf16[1536,128]{1,0:T(8,128)(2,1)} %pad_maximum_fusion), channel_id=1, source_target_pairs={{0,1},{1,0},{2,3},{3,2},{4,5},{5,4},{6,7},{7,6},{8,9},{9,8},{10,11... | collective-permute-start | bytes 1179656 | tf_op jit(solution)/shard_map/ppermute | solution.py:105
  59.9 0.9 slice_negate_fusion.1
  61.3 1.3 %copy.50 = bf16[28,8,24,128]{3,1,2,0:T(8,128)(2,1)} copy(bf16[28,8,24,128]{3,2,1,0:T(8,128)(2,1)S(1)} %bitcast.33) | data formatting | bytes 2752512
  62.6 2.5 %fusion.28 = (f32[512]{0:T(512)S(1)}, f32[512,1536]{1,0:T(8,128)S(1)}) fusion(bf16[1536,128]{1,0:T(8,128)(2,1)} %pad_maximum_fusion, bf16[1536,128]{1,0:T(8,128)(2,1)} %collective-permute-done.2, pred[]{:T(512)S(6)} %eq.3, f32[512,64]{1,0:T(8,128)S(1)} %copy-done.4, f32[512,64]{1,0:T(8,128)S(1)} %copy-done.3, f32[512,128]{1,0:T(8,128)S(1)} %multiply_multiply_fusion.1, ...), kind=kOutput, calls=%fused_computation.61 | convolution fusion | flops 207552000 | bytes 4730369 | tf_op jit(solution)/shard_map/dot_general | solution.py:121
  65.6 1.7 %fusion.8 = bf16[512,128]{1,0:T(8,128)(2,1)S(1)} fusion(f32[512,1536]{1,0:T(8,128)S(1)} %get-tuple-element.26, f32[512]{0:T(512)S(1)} %fusion.5, f32[512]{0:T(512)S(1)} %get-tuple-element.25, bf16[1536,128]{1,0:T(8,128)(2,1)} %collective-permute-done.2, bf16[1536,128]{1,0:T(8,128)(2,1)} %pad_maximum_fusion, pred[]{:T(512)S(6)} %eq.3), kind=kOutput, calls=%fused_computation.19 | convolution fusion | flops 203948032 | bytes 4067329 | tf_op jit(solution)/shard_map/dot_general | solution.py:131
  67.6 36.5 %all_to_all.26 = bf16[12,512,128]{2,1,0:T(8,128)(2,1)} all-to-all(bf16[12,512,128]{2,1,0:T(8,128)(2,1)S(1)} %broadcast_in_dim.8), channel_id=1, replica_groups=mesh['ctx'=32,'zl'=3,'x'=4,'core'=2] {'zl','x'}, dimensions={0} | all-to-all | bytes 3145728 | tf_op jit(solution)/shard_map/all_to_all | solution.py:137
  104.2 2.1 %collective-permute-start.3 = (bf16[12,512,128]{2,1,0:T(8,128)(2,1)}, bf16[12,512,128]{2,1,0:T(8,128)(2,1)}, u32[]{:S(2)}, u32[]{:S(2)}) collective-permute-start(bf16[12,512,128]{2,1,0:T(8,128)(2,1)} %all_to_all.26), channel_id=1, source_target_pairs={{0,1},{1,0},{2,3},{3,2},{4,5},{5,4},{6,7},{7,6},{8,9},{9,8},{10,11... | collective-permute-start | bytes 4718600 | tf_op jit(solution)/shard_map/ppermute | solution.py:138
  106.3 3.7 %reshape.78 = bf16[12,2,128,224]{2,1,0,3:T(2,128)(2,1)S(1)} reshape(bf16[3072,224]{0,1:T(8,128)(2,1)} %bitcast.32) | data formatting | bytes 2752512 | tf_op jit(solution)/shard_map/reshape | solution.py:139
  110.0 3.3 %broadcast_select_fusion = (bf16[12,1,128,224]{2,1,0,3:T(2,128)(2,1)S(1)}, bf16[12,1,128,224]{2,1,0,3:T(2,128)(2,1)S(1)}) fusion(pred[]{:T(512)S(6)} %eq.3, bf16[12,2,128,224]{2,1,0,3:T(2,128)(2,1)S(1)} %reshape.78), kind=kLoop, calls=%fused_computation.12 | loop fusion | flops 688128 | bytes 2752513 | tf_op jit(solution)/shard_map/jit(_where)/select_n | solution.py:141
  113.2 2.0 %convolution_bitcast_fusion.1 = f32[512,224]{0,1:T(8,128)S(1)} fusion(bf16[12,512,128]{2,1,0:T(8,128)(2,1)} %all_to_all.26, bf16[12,1,128,224]{2,1,0,3:T(2,128)(2,1)S(1)} %get-tuple-element.16), kind=kOutput, calls=%fused_computation.17 | convolution fusion | flops 352321536 | bytes 2719744 | tf_op jit(solution)/shard_map/dot_general | solution.py:143
  115.3 2.1 %multiply_reduce_fusion = (f32[512]{0:T(512)S(1)}, f32[512,224]{0,1:T(8,128)S(1)}) fusion(f32[512,224]{0,1:T(8,128)S(1)} %convolution_bitcast_fusion.1, bf16[12,512,128]{2,1,0:T(8,128)(2,1)} %collective-permute-done.3, bf16[12,1,128,224]{2,1,0,3:T(2,128)(2,1)S(1)} %get-tuple-element.15), kind=kOutput, calls=%fused_computation.25 | convolution fusion | flops 352665088 | bytes 3180544 | tf_op jit(solution)/shard_map/dot_general | solution.py:145
  117.4 0.7 broadcast_in_dim.9
  118.0 4.9 %all-to-all-start.2 = ((f32[24,1,512]{2,1,0:T(1,128)}), f32[24,1,512]{2,1,0:T(1,128)S(1)}, u32[]{:S(2)}, u32[]{:S(2)}) async-start(f32[24,1,512]{2,1,0:T(1,128)} %broadcast_in_dim.9), calls=%async_computation.2 | async-start | bytes 98304 | tf_op jit(solution)/shard_map/all_to_all | solution.py:148
  122.9 1.1 constant_dynamic-slice_fusion
  124.2 5.8 %all-to-all-done.2 = f32[24,1,512]{2,1,0:T(1,128)S(1)} async-done(((f32[24,1,512]{2,1,0:T(1,128)}), f32[24,1,512]{2,1,0:T(1,128)S(1)}, u32[]{:S(2)}, u32[]{:S(2)}) %all-to-all-start.2) | async-done | bytes 49184 | tf_op jit(solution)/shard_map/all_to_all | solution.py:148
  130.0 0.8 add_convert_fusion
  (35 shorter events, 1.9 us)
Async XLA Ops:
  0.0 41.2 %copy-start = (bf16[5376,128]{1,0:T(8,128)(2,1)S(1)}, bf16[5376,128]{1,0:T(8,128)(2,1)}, u32[]{:S(2)}) copy-start(bf16[5376,128]{1,0:T(8,128)(2,1)} %param.10) | copy-start | bytes 4128772
  2.6 8.3 %copy-start.5 = (f32[5376]{0:T(1024)S(1)}, f32[5376]{0:T(1024)}, u32[]{:S(2)}) copy-start(f32[5376]{0:T(1024)} %param.9) | copy-start | bytes 64516
  2.6 58.1 %all-to-all-start = ((bf16[128,24,224]{0,2,1:T(8,128)(2,1)}), bf16[128,24,224]{0,2,1:T(8,128)(2,1)S(1)}, u32[]{:S(2)}, u32[]{:S(2)}) async-start(bf16[128,24,224]{0,2,1:T(8,128)(2,1)} %bitcast.31), calls=%async_computation | async-start | bytes 2752512 | tf_op jit(solution)/shard_map/all_to_all | solution.py:99
  11.6 7.7 %copy-start.6 = (f32[128]{0:T(128)S(1)}, f32[128]{0:T(128)}, u32[]{:S(2)}) copy-start(f32[128]{0:T(128)} %param.13) | copy-start | bytes 1540
  18.1 3.4 %copy-start.1 = (f32[512,128]{1,0:T(8,128)S(1)}, f32[512,128]{1,0:T(8,128)}, u32[]{:S(2)}) copy-start(f32[512,128]{1,0:T(8,128)} %get-tuple-element.11) | copy-start | bytes 786436
  20.4 20.7 %copy-start.2 = (f32[512,1]{1,0:T(8,128)S(1)}, f32[512,1]{1,0:T(8,128)}, u32[]{:S(2)}) copy-start(f32[512,1]{1,0:T(8,128)} %get-tuple-element.10) | copy-start | bytes 6148
  22.5 29.4 %collective-permute-start = (bf16[512,128]{1,0:T(8,128)(2,1)}, bf16[512,128]{1,0:T(8,128)(2,1)}, u32[]{:S(2)}, u32[]{:S(2)}) collective-permute-start(bf16[512,128]{1,0:T(8,128)(2,1)} %fusion.22), channel_id=1, source_target_pairs={{0,48},{24,72},{48,96},{72,120},{96,144},{120,168},{144,192},{168,... | collective-permute-start | bytes 393224 | tf_op jit(solution)/shard_map/ppermute | solution.py:20
  36.5 19.6 %collective-permute-start.1 = (bf16[512,128]{1,0:T(8,128)(2,1)}, bf16[512,128]{1,0:T(8,128)(2,1)}, u32[]{:S(2)}, u32[]{:S(2)}) collective-permute-start(bf16[512,128]{1,0:T(8,128)(2,1)} %fusion.22), channel_id=1, source_target_pairs={{0,24},{24,48},{48,72},{72,96},{96,120},{120,144},{144,168},{168,1... | collective-permute-start | bytes 393224 | tf_op jit(solution)/shard_map/ppermute | solution.py:20
  41.2 5.5 %copy-start.8 = (f32[128]{0:T(128)S(1)}, f32[128]{0:T(128)}, u32[]{:S(2)}) copy-start(f32[128]{0:T(128)} %param.12) | copy-start | bytes 1540
  57.9 4.7 %collective-permute-start.2 = (bf16[1536,128]{1,0:T(8,128)(2,1)}, bf16[1536,128]{1,0:T(8,128)(2,1)}, u32[]{:S(2)}, u32[]{:S(2)}) collective-permute-start(bf16[1536,128]{1,0:T(8,128)(2,1)} %pad_maximum_fusion), channel_id=1, source_target_pairs={{0,1},{1,0},{2,3},{3,2},{4,5},{5,4},{6,7},{7,6},{8,9},{9,8},{10,11... | collective-permute-start | bytes 1179656 | tf_op jit(solution)/shard_map/ppermute | solution.py:105
  61.3 1.3 %copy-start.3 = (f32[512,64]{1,0:T(8,128)S(1)}, f32[512,64]{1,0:T(8,128)}, u32[]{:S(2)}) copy-start(f32[512,64]{1,0:T(8,128)} %get-tuple-element.17) | copy-start | bytes 393220
  61.3 1.3 %copy-start.4 = (f32[512,64]{1,0:T(8,128)S(1)}, f32[512,64]{1,0:T(8,128)}, u32[]{:S(2)}) copy-start(f32[512,64]{1,0:T(8,128)} %get-tuple-element.18) | copy-start | bytes 393220
  104.2 11.1 %collective-permute-start.3 = (bf16[12,512,128]{2,1,0:T(8,128)(2,1)}, bf16[12,512,128]{2,1,0:T(8,128)(2,1)}, u32[]{:S(2)}, u32[]{:S(2)}) collective-permute-start(bf16[12,512,128]{2,1,0:T(8,128)(2,1)} %all_to_all.26), channel_id=1, source_target_pairs={{0,1},{1,0},{2,3},{3,2},{4,5},{5,4},{6,7},{7,6},{8,9},{9,8},{10,11... | collective-permute-start | bytes 4718600 | tf_op jit(solution)/shard_map/ppermute | solution.py:138
  115.3 14.7 %copy-start.7 = (f32[224]{0:T(256)S(1)}, f32[224]{0:T(256)}, u32[]{:S(2)}) copy-start(f32[224]{0:T(256)} %param.15) | copy-start | bytes 2692
  118.0 11.9 %all-to-all-start.2 = ((f32[24,1,512]{2,1,0:T(1,128)}), f32[24,1,512]{2,1,0:T(1,128)S(1)}, u32[]{:S(2)}, u32[]{:S(2)}) async-start(f32[24,1,512]{2,1,0:T(1,128)} %broadcast_in_dim.9), calls=%async_computation.2 | async-start | bytes 98304 | tf_op jit(solution)/shard_map/all_to_all | solution.py:148

commit v3 on v0

--- a/solution.py
+++ b/solution.py
@@ -2,6 +2,7 @@
 import jax.numpy as jnp
 from jax import lax
 from jax.sharding import Mesh, PartitionSpec as P
+
 
 WIN = 1024
 
@@ -11,7 +12,6 @@
 rope_base = 10000.0
 
 TP_AXES = ("zl", "x", "core")
-Z_HI = 4
 
 
 def from_behind(block, axis, distance):
@@ -72,15 +72,7 @@
         out_weight.reshape(head_width, n_tp, col_share), TP_AXES, 1, 0, tiled=True
     ).reshape(n_tp * head_width, col_share)
     span_count = WIN // tok_rows
-    n_ctx = lax.axis_size("ctx")
-    devices = range(n_ctx)
-    mid = [(c // Z_HI) * Z_HI + (c % Z_HI - 1) % Z_HI for c in devices]
-    first_leg = [(c, mid[c]) for c in devices if c + span_count in devices]
-    second_leg = [(mid[c], c + span_count) for c in devices if c + span_count in devices]
-    far_block = lax.ppermute(lax.ppermute(own_block, "ctx", first_leg), "ctx", second_leg)
-    earlier = [far_block] + [
-        from_behind(own_block, "ctx", offset) for offset in range(span_count - 1, 0, -1)
-    ]
+    earlier = [from_behind(own_block, "ctx", offset) for offset in range(span_count, 0, -1)]
     own_window = jnp.concatenate(earlier + [own_block], axis=0)
     other_window = lax.ppermute(own_window, "core", [(0, 1), (1, 0)])
     weight_block, own_window, other_window = lax.optimization_barrier(

time: 134 us -> 131 us (0.978)
  the two profiles are of different devices: /device:TPU:33 before, /device:TPU:56 now
where the time goes in v3:
time: 131 us; the launch traced here: 130 us
  blocking collectives  37.4 us (29%)
  starting transfers between devices  35.5 us (27%)
  matrix products  17.9 us (14%)
  waiting for transfers between devices  17.1 us (13%)
  other arithmetic  11 us (8%)
  local copies, waits for them, and re-layouts  10.4 us (8%)
    all_to_all x1, blocking collectives, layer(): own_heads = lax.all_to_all(copies, ('zl', 'x'), 0, 0, tiled=True)  37.4 us
    ppermute x2, starting transfers between devices, from_behind(): return lax.ppermute(block, axis, route)  18.5 us
    ppermute x2, waiting for transfers between devices, from_behind(): return lax.ppermute(block, axis, route)  11.3 us
    all_to_all x1, starting transfers between devices, layer(): lax.all_to_all(out_weight.reshape(head_width, n_tp, col_share), TP_AXES,...  8.17 us
    all_to_all x1, waiting for transfers between devices, layer(): lax.all_to_all(square_copies, TP_AXES, 0, 0, tiled=True)  5.75 us
    dot_general x1, matrix products, layer(): queries = jnp.dot(normed, query_weight, preferred_element_type=jnp.float32)  5.02 us
    all_to_all x1, starting transfers between devices, layer(): lax.all_to_all(square_copies, TP_AXES, 0, 0, tiled=True)  4.78 us
    dot_general x1, matrix products, layer(): jnp.dot(normed, keyval_weight, preferred_element_type=jnp.float32)  4.63 us
  transfers between devices with their start and end apart: 6, of which 4 were waited for; matrix products, arithmetic and copies ran while one was open for 22% of the time, Pallas kernels for 0%

profile of v3, /device:TPU:56, one launch (start us, length us, event | category | flops | bytes accessed | tf_op | source)
XLA Modules:
  0.0 129.6 jit_solution(16543850946128905283)
XLA Ops:
  0.0 2.6 %copy.26 = bf16[128,5376]{0,1:T(8,128)(2,1)} copy(bf16[128,5376]{1,0:T(8,128)(2,1)} %param.14) | data formatting | bytes 2752512 | tf_op args[6]
  2.6 8.2 %all-to-all-start = ((bf16[128,24,224]{0,2,1:T(8,128)(2,1)}), bf16[128,24,224]{0,2,1:T(8,128)(2,1)S(1)}, u32[]{:S(2)}, u32[]{:S(2)}) async-start(bf16[128,24,224]{0,2,1:T(8,128)(2,1)} %bitcast.32), calls=%async_computation | async-start | bytes 2752512 | tf_op jit(solution)/shard_map/all_to_all | solution.py:71
  10.8 3.7 %fusion = f32[512]{0:T(512)S(1)} fusion(bf16[512,5376]{1,0:T(8,128)(2,1)} %param.8), kind=kLoop, calls=%fused_computation.2 | loop fusion | flops 8257024 | bytes 5507072 | tf_op jit(solution)/shard_map/reduce_sum | solution.py:42
  14.6 4.6 %multiply_reduce_fusion.1 = (f32[512]{0:T(512)S(1)}, f32[512,128]{0,1:T(8,128)S(1)}) fusion(bf16[5376,128]{1,0:T(8,128)(2,1)S(1)} %copy-done, bf16[512,5376]{1,0:T(8,128)(2,1)} %param.8, f32[5376]{0:T(1024)S(1)} %copy-done.4, f32[512]{0:T(512)S(1)} %add_rsqrt_fusion.3), kind=kOutput, calls=%fused_computation.47 | convolution fusion | flops 715783680 | bytes 7169024 | tf_op jit(solution)/shard_map/dot_general | solution.py:67
  19.2 0.5 multiply_sine_fusion
  19.9 0.1 fusion.28
  20.0 13.9 %collective-permute-start = (bf16[512,128]{0,1:T(8,128)(2,1)S(1)}, bf16[512,128]{0,1:T(8,128)(2,1)S(1)}, u32[]{:S(2)}, u32[]{:S(2)}) collective-permute-start(bf16[512,128]{0,1:T(8,128)(2,1)S(1)} %fusion.28), channel_id=1, source_target_pairs={{0,48},{24,72},{48,96},{72,120},{96,144},{120,168},{144,192},{168,... | collective-permute-start | bytes 393224 | tf_op jit(solution)/shard_map/ppermute | solution.py:20
  34.0 4.6 %collective-permute-start.1 = (bf16[512,128]{0,1:T(8,128)(2,1)S(1)}, bf16[512,128]{0,1:T(8,128)(2,1)}, u32[]{:S(2)}, u32[]{:S(2)}) collective-permute-start(bf16[512,128]{0,1:T(8,128)(2,1)S(1)} %fusion.28), channel_id=1, source_target_pairs={{0,24},{24,48},{48,72},{72,96},{96,120},{120,144},{144,168},{168,1... | collective-permute-start | bytes 393224 | tf_op jit(solution)/shard_map/ppermute | solution.py:20
  38.6 5.0 %multiply_reduce_fusion.2 = (f32[512]{0:T(512)S(1)}, f32[512,128]{0,1:T(8,128)S(1)}) fusion(bf16[5376,128]{1,0:T(8,128)(2,1)} %param.10, bf16[512,5376]{1,0:T(8,128)(2,1)} %param.8, f32[5376]{0:T(1024)S(1)} %copy-done.4, f32[512]{0:T(512)S(1)} %add_rsqrt_fusion.3), kind=kOutput, calls=%fused_computation.49 | convolution fusion | flops 715783680 | bytes 7169024 | tf_op jit(solution)/shard_map/dot_general | solution.py:84
  43.7 9.7 %collective-permute-done = bf16[512,128]{0,1:T(8,128)(2,1)S(1)} collective-permute-done((bf16[512,128]{0,1:T(8,128)(2,1)S(1)}, bf16[512,128]{0,1:T(8,128)(2,1)S(1)}, u32[]{:S(2)}, u32[]{:S(2)}) %collective-permute-start) | collective-permute-done | bytes 131104 | tf_op jit(solution)/shard_map/ppermute | solution.py:20
  53.4 1.6 %collective-permute-done.1 = bf16[512,128]{0,1:T(8,128)(2,1)} collective-permute-done((bf16[512,128]{0,1:T(8,128)(2,1)S(1)}, bf16[512,128]{0,1:T(8,128)(2,1)}, u32[]{:S(2)}, u32[]{:S(2)}) %collective-permute-start.1) | collective-permute-done | bytes 131104 | tf_op jit(solution)/shard_map/ppermute | solution.py:20
  55.0 1.7 %pad_maximum_fusion = bf16[1536,128]{0,1:T(8,128)(2,1)} fusion(bf16[512,128]{0,1:T(8,128)(2,1)S(1)} %fusion.28, bf16[512,128]{0,1:T(8,128)(2,1)} %collective-permute-done.1, bf16[512,128]{0,1:T(8,128)(2,1)S(1)} %collective-permute-done), kind=kLoop, calls=%fused_computation.29 | loop fusion | flops 1179648 | bytes 786432 | tf_op jit(solution)/shard_map/concatenate | solution.py:76
  56.7 1.9 %collective-permute-start.2 = (bf16[1536,128]{0,1:T(8,128)(2,1)}, bf16[1536,128]{0,1:T(8,128)(2,1)}, u32[]{:S(2)}, u32[]{:S(2)}) collective-permute-start(bf16[1536,128]{0,1:T(8,128)(2,1)} %pad_maximum_fusion), channel_id=1, source_target_pairs={{0,1},{1,0},{2,3},{3,2},{4,5},{5,4},{6,7},{7,6},{8,9},{9,8},{10,11... | collective-permute-start | bytes 1179656 | tf_op jit(solution)/shard_map/ppermute | solution.py:77
  58.7 0.5 copy.27
  59.2 1.3 %copy.45 = bf16[28,8,24,128]{3,1,2,0:T(8,128)(2,1)} copy(bf16[28,8,24,128]{3,2,1,0:T(8,128)(2,1)S(1)} %bitcast.34) | data formatting | bytes 2752512
  60.6 0.1 collective-permute-done.2
  60.7 2.4 %fusion.35 = (f32[512]{0:T(512)S(1)}, f32[512,1536]{1,0:T(8,128)S(1)}) fusion(bf16[1536,128]{0,1:T(8,128)(2,1)} %pad_maximum_fusion, bf16[1536,128]{0,1:T(8,128)(2,1)} %collective-permute-done.2, pred[]{:T(512)S(6)} %eq.3, f32[512,128]{0,1:T(8,128)S(1)} %multiply_multiply_fusion.1, f32[512,64]{0,1:T(8,128)S(1)} %get-tuple-element.18, ...), kind=kOutput, calls=%fused_computation.67 | convolution fusion | flops 207552000 | bytes 4730369 | tf_op jit(solution)/shard_map/dot_general | solution.py:92
  63.0 0.6 fusion.5
  63.6 1.7 %fusion.12 = bf16[512,128]{1,0:T(8,128)(2,1)S(1)} fusion(f32[512,1536]{1,0:T(8,128)S(1)} %get-tuple-element.24, f32[512]{0:T(512)S(1)} %fusion.5, f32[512]{0:T(512)S(1)} %get-tuple-element.23, bf16[1536,128]{0,1:T(8,128)(2,1)} %collective-permute-done.2, bf16[1536,128]{0,1:T(8,128)(2,1)} %pad_maximum_fusion, pred[]{:T(512)S(6)} %eq.3), kind=kOutput, calls=%fused_computation.22 | convolution fusion | flops 203948032 | bytes 4067329 | tf_op jit(solution)/shard_map/dot_general | solution.py:102
  65.3 0.3 broadcast_in_dim.8
  65.6 37.4 %all_to_all.26 = bf16[12,512,128]{2,1,0:T(8,128)(2,1)} all-to-all(bf16[12,512,128]{2,1,0:T(8,128)(2,1)S(1)} %broadcast_in_dim.8), channel_id=1, replica_groups=mesh['ctx'=32,'zl'=3,'x'=4,'core'=2] {'zl','x'}, dimensions={0} | all-to-all | bytes 3145728 | tf_op jit(solution)/shard_map/all_to_all | solution.py:108
  103.0 2.1 %collective-permute-start.3 = (bf16[12,512,128]{2,1,0:T(8,128)(2,1)}, bf16[12,512,128]{2,1,0:T(8,128)(2,1)}, u32[]{:S(2)}, u32[]{:S(2)}) collective-permute-start(bf16[12,512,128]{2,1,0:T(8,128)(2,1)} %all_to_all.26), channel_id=1, source_target_pairs={{0,1},{1,0},{2,3},{3,2},{4,5},{5,4},{6,7},{7,6},{8,9},{9,8},{10,11... | collective-permute-start | bytes 4718600 | tf_op jit(solution)/shard_map/ppermute | solution.py:109
  105.1 3.7 %reshape.82 = bf16[12,2,128,224]{2,1,0,3:T(2,128)(2,1)S(1)} reshape(bf16[3072,224]{0,1:T(8,128)(2,1)} %bitcast.33) | data formatting | bytes 2752512 | tf_op jit(solution)/shard_map/reshape | solution.py:110
  108.8 3.3 %broadcast_select_fusion = (bf16[12,1,128,224]{2,1,0,3:T(2,128)(2,1)S(1)}, bf16[12,1,128,224]{2,1,0,3:T(2,128)(2,1)S(1)}) fusion(pred[]{:T(512)S(6)} %eq.3, bf16[12,2,128,224]{2,1,0,3:T(2,128)(2,1)S(1)} %reshape.82), kind=kLoop, calls=%fused_computation.13 | loop fusion | flops 688128 | bytes 2752513 | tf_op jit(solution)/shard_map/jit(_where)/select_n | solution.py:112
  112.1 2.1 %convolution_bitcast_fusion.1 = f32[512,224]{0,1:T(8,128)S(1)} fusion(bf16[12,512,128]{2,1,0:T(8,128)(2,1)} %all_to_all.26, bf16[12,1,128,224]{2,1,0,3:T(2,128)(2,1)S(1)} %get-tuple-element.12), kind=kOutput, calls=%fused_computation.20 | convolution fusion | flops 352321536 | bytes 2719744 | tf_op jit(solution)/shard_map/dot_general | solution.py:114
  114.2 2.1 %multiply_reduce_fusion = (f32[512]{0:T(512)S(1)}, f32[512,224]{0,1:T(8,128)S(1)}) fusion(f32[512,224]{0,1:T(8,128)S(1)} %convolution_bitcast_fusion.1, bf16[12,512,128]{2,1,0:T(8,128)(2,1)} %collective-permute-done.3, bf16[12,1,128,224]{2,1,0,3:T(2,128)(2,1)S(1)} %get-tuple-element.11), kind=kOutput, calls=%fused_computation.28 | convolution fusion | flops 352665088 | bytes 3180544 | tf_op jit(solution)/shard_map/dot_general | solution.py:116
  116.3 0.7 broadcast_in_dim.9
  116.9 4.8 %all-to-all-start.2 = ((f32[24,1,512]{2,1,0:T(1,128)}), f32[24,1,512]{2,1,0:T(1,128)S(1)}, u32[]{:S(2)}, u32[]{:S(2)}) async-start(f32[24,1,512]{2,1,0:T(1,128)} %broadcast_in_dim.9), calls=%async_computation.2 | async-start | bytes 98304 | tf_op jit(solution)/shard_map/all_to_all | solution.py:119
  121.7 1.1 constant_dynamic-slice_fusion
  122.9 0.1 copy.32
  123.0 5.8 %all-to-all-done.2 = f32[24,1,512]{2,1,0:T(1,128)S(1)} async-done(((f32[24,1,512]{2,1,0:T(1,128)}), f32[24,1,512]{2,1,0:T(1,128)S(1)}, u32[]{:S(2)}, u32[]{:S(2)}) %all-to-all-start.2) | async-done | bytes 49184 | tf_op jit(solution)/shard_map/all_to_all | solution.py:119
  128.8 0.8 add_convert_fusion
  (25 shorter events, 0.4 us)
Async XLA Ops:
  0.0 14.6 %copy-start = (bf16[5376,128]{1,0:T(8,128)(2,1)S(1)}, bf16[5376,128]{1,0:T(8,128)(2,1)}, u32[]{:S(2)}) copy-start(bf16[5376,128]{1,0:T(8,128)(2,1)} %param.11) | copy-start | bytes 4128772
  2.6 56.1 %all-to-all-start = ((bf16[128,24,224]{0,2,1:T(8,128)(2,1)}), bf16[128,24,224]{0,2,1:T(8,128)(2,1)S(1)}, u32[]{:S(2)}, u32[]{:S(2)}) async-start(bf16[128,24,224]{0,2,1:T(8,128)(2,1)} %bitcast.32), calls=%async_computation | async-start | bytes 2752512 | tf_op jit(solution)/shard_map/all_to_all | solution.py:71
  10.8 3.8 %copy-start.4 = (f32[5376]{0:T(1024)S(1)}, f32[5376]{0:T(1024)}, u32[]{:S(2)}) copy-start(f32[5376]{0:T(1024)} %param.9) | copy-start | bytes 64516
  14.6 5.2 %copy-start.1 = (f32[128]{0:T(128)S(1)}, f32[128]{0:T(128)}, u32[]{:S(2)}) copy-start(f32[128]{0:T(128)} %param.13) | copy-start | bytes 1540
  20.0 33.4 %collective-permute-start = (bf16[512,128]{0,1:T(8,128)(2,1)S(1)}, bf16[512,128]{0,1:T(8,128)(2,1)S(1)}, u32[]{:S(2)}, u32[]{:S(2)}) collective-permute-start(bf16[512,128]{0,1:T(8,128)(2,1)S(1)} %fusion.28), channel_id=1, source_target_pairs={{0,48},{24,72},{48,96},{72,120},{96,144},{120,168},{144,192},{168,... | collective-permute-start | bytes 393224 | tf_op jit(solution)/shard_map/ppermute | solution.py:20
  34.0 21.0 %collective-permute-start.1 = (bf16[512,128]{0,1:T(8,128)(2,1)S(1)}, bf16[512,128]{0,1:T(8,128)(2,1)}, u32[]{:S(2)}, u32[]{:S(2)}) collective-permute-start(bf16[512,128]{0,1:T(8,128)(2,1)S(1)} %fusion.28), channel_id=1, source_target_pairs={{0,24},{24,48},{48,72},{72,96},{96,120},{120,144},{144,168},{168,1... | collective-permute-start | bytes 393224 | tf_op jit(solution)/shard_map/ppermute | solution.py:20
  38.6 5.1 %copy-start.3 = (f32[128]{0:T(128)S(1)}, f32[128]{0:T(128)}, u32[]{:S(2)}) copy-start(f32[128]{0:T(128)} %param.12) | copy-start | bytes 1540
  56.7 3.9 %collective-permute-start.2 = (bf16[1536,128]{0,1:T(8,128)(2,1)}, bf16[1536,128]{0,1:T(8,128)(2,1)}, u32[]{:S(2)}, u32[]{:S(2)}) collective-permute-start(bf16[1536,128]{0,1:T(8,128)(2,1)} %pad_maximum_fusion), channel_id=1, source_target_pairs={{0,1},{1,0},{2,3},{3,2},{4,5},{5,4},{6,7},{7,6},{8,9},{9,8},{10,11... | collective-permute-start | bytes 1179656 | tf_op jit(solution)/shard_map/ppermute | solution.py:77
  103.0 11.2 %collective-permute-start.3 = (bf16[12,512,128]{2,1,0:T(8,128)(2,1)}, bf16[12,512,128]{2,1,0:T(8,128)(2,1)}, u32[]{:S(2)}, u32[]{:S(2)}) collective-permute-start(bf16[12,512,128]{2,1,0:T(8,128)(2,1)} %all_to_all.26), channel_id=1, source_target_pairs={{0,1},{1,0},{2,3},{3,2},{4,5},{5,4},{6,7},{7,6},{8,9},{9,8},{10,11... | collective-permute-start | bytes 4718600 | tf_op jit(solution)/shard_map/ppermute | solution.py:109
  112.1 16.7 %copy-start.2 = (f32[224]{0:T(256)S(1)}, f32[224]{0:T(256)}, u32[]{:S(2)}) copy-start(f32[224]{0:T(256)} %param.15) | copy-start | bytes 2692
  116.9 11.8 %all-to-all-start.2 = ((f32[24,1,512]{2,1,0:T(1,128)}), f32[24,1,512]{2,1,0:T(1,128)S(1)}, u32[]{:S(2)}, u32[]{:S(2)}) async-start(f32[24,1,512]{2,1,0:T(1,128)} %broadcast_in_dim.9), calls=%async_computation.2 | async-start | bytes 98304 | tf_op jit(solution)/shard_map/all_to_all | solution.py:119

commit v4 on v3

--- a/solution.py
+++ b/solution.py
@@ -64,7 +64,12 @@
     positions = ctx_index * tok_rows + jnp.arange(tok_rows, dtype=jnp.int32)
     cosine, sine_table = rope_tables(positions, head_width)
 
-    projected = jnp.dot(normed, keyval_weight, preferred_element_type=jnp.float32)
+    both = jnp.dot(
+        normed,
+        jnp.concatenate([keyval_weight, query_weight], axis=1),
+        preferred_element_type=jnp.float32,
+    )
+    projected = both[:, :head_width]
     rotated = rotate(rms_scale(projected, key_gain), cosine, sine_table)
     own_block = jnp.where(is_even, rotated, projected).astype(jnp.bfloat16)
     n_tp = n_zl * n_x * n_core
@@ -81,7 +86,7 @@
     key_window = jnp.where(is_even, own_window, other_window)
     value_window = jnp.where(is_even, other_window, own_window)
 
-    queries = jnp.dot(normed, query_weight, preferred_element_type=jnp.float32)
+    queries = both[:, head_width:]
     queries = (
         rotate(rms_scale(queries, query_gain), cosine, sine_table) * query_scalar ** (-0.5)
     ).astype(jnp.bfloat16)

time: 131 us -> 126 us (0.962)
  waiting for transfers between devices: 17.1 us -> 26.7 us
  matrix products: 17.9 us -> 11.6 us
  local copies, waits for them, and re-layouts: 10.4 us -> 6.77 us
  blocking collectives: 37.4 us -> 34.6 us
    ppermute x2, waiting for transfers between devices: 11.3 us -> 19.7 us  [from_behind(): return lax.ppermute(block, axis, route)]
    dot_general x2 -> x1, matrix products: 9.65 us -> 3.37 us  [layer(): jnp.dot(normed, jnp.concatenate([keyval_weight, query_weight], axis=1), p...]
    all_to_all x1, blocking collectives: 37.4 us -> 34.6 us  [layer(): own_heads = lax.all_to_all(copies, ('zl', 'x'), 0, 0, tiled=True)]
    reshape x1, local copies, waits for them, and re-layouts: 3.69 us -> 1.01 us  [layer(): rows = weight_block.reshape(n_peer, n_core, head_width, col_share)]
    unnamed x13 -> x15, local copies, waits for them, and re-layouts: 4.08 us -> 3.18 us
    reduce_sum x1 -> x2, other arithmetic: 3.72 us -> 3.93 us  [rms_scale(): jnp.mean(signal * signal, axis=-1, keepdims=True) + epsilon]
  transfers between devices with their start and end apart: 6 -> 6, of which waited for: 4 -> 4; matrix products, arithmetic and copies ran while one was open for 22% -> 14% of each run, Pallas kernels for 0% -> 0%
where the time goes in v4:
time: 126 us; the launch traced here: 125 us
  starting transfers between devices  35.2 us (28%)
  blocking collectives  34.6 us (27%)
  waiting for transfers between devices  26.7 us (21%)
  matrix products  11.6 us (9%)
  other arithmetic  10.3 us (8%)
  local copies, waits for them, and re-layouts  6.77 us (5%)
    all_to_all x1, blocking collectives, layer(): own_heads = lax.all_to_all(copies, ('zl', 'x'), 0, 0, tiled=True)  34.6 us
    ppermute x2, waiting for transfers between devices, from_behind(): return lax.ppermute(block, axis, route)  19.7 us
    ppermute x2, starting transfers between devices, from_behind(): return lax.ppermute(block, axis, route)  18.5 us
    all_to_all x1, starting transfers between devices, layer(): lax.all_to_all(out_weight.reshape(head_width, n_tp, col_share), TP_AXES,...  8.3 us
    all_to_all x1, waiting for transfers between devices, layer(): lax.all_to_all(square_copies, TP_AXES, 0, 0, tiled=True)  5.75 us
    all_to_all x1, starting transfers between devices, layer(): lax.all_to_all(square_copies, TP_AXES, 0, 0, tiled=True)  4.5 us
    reduce_sum x2, other arithmetic, rms_scale(): jnp.mean(signal * signal, axis=-1, keepdims=True) + epsilon  3.93 us
    dot_general x1, matrix products, layer(): jnp.dot(normed, jnp.concatenate([keyval_weight, query_weight], axis=1), p...  3.37 us
  transfers between devices with their start and end apart: 6, of which 4 were waited for; matrix products, arithmetic and copies ran while one was open for 14% of the time, Pallas kernels for 0%

profile of v4, /device:TPU:56, one launch (start us, length us, event | category | flops | bytes accessed | tf_op | source)
XLA Modules:
  0.0 125.4 jit_solution(10212980413907122651)
XLA Ops:
  0.0 2.5 %copy.26 = bf16[128,5376]{0,1:T(8,128)(2,1)} copy(bf16[128,5376]{1,0:T(8,128)(2,1)} %param.14) | data formatting | bytes 2752512 | tf_op args[6]
  2.5 8.3 %all-to-all-start = ((bf16[128,24,224]{0,2,1:T(8,128)(2,1)}), bf16[128,24,224]{0,2,1:T(8,128)(2,1)S(1)}, u32[]{:S(2)}, u32[]{:S(2)}) async-start(bf16[128,24,224]{0,2,1:T(8,128)(2,1)} %bitcast), calls=%async_computation | async-start | bytes 2752512 | tf_op jit(solution)/shard_map/all_to_all | solution.py:76
  10.9 3.9 %fusion = f32[512]{0:T(512)S(1)} fusion(bf16[512,5376]{1,0:T(8,128)(2,1)} %param.8), kind=kLoop, calls=%fused_computation.2 | loop fusion | flops 8257024 | bytes 5507072 | tf_op jit(solution)/shard_map/reduce_sum | solution.py:42
  14.7 0.3 copy-done
  15.0 3.4 %fusion.3 = f32[512,256]{0,1:T(8,128)S(1)} fusion(bf16[512,5376]{1,0:T(8,128)(2,1)S(1)} %copy-done, f32[5376]{0:T(1024)S(1)} %copy-done.5, f32[512]{0:T(512)S(1)} %add_rsqrt_fusion.3, bf16[5376,128]{1,0:T(8,128)(2,1)S(1)} %copy-done.4, bf16[5376,128]{1,0:T(8,128)(2,1)} %param.11), kind=kOutput, calls=%fused_computation.5 | convolution fusion | flops 1425801216 | bytes 8805376 | tf_op jit(solution)/shard_map/dot_general | solution.py:67
  18.5 0.5 multiply_sine_fusion
  19.2 0.1 fusion.31
  19.3 13.9 %collective-permute-start = (bf16[512,128]{0,1:T(8,128)(2,1)S(1)}, bf16[512,128]{0,1:T(8,128)(2,1)S(1)}, u32[]{:S(2)}, u32[]{:S(2)}) collective-permute-start(bf16[512,128]{0,1:T(8,128)(2,1)S(1)} %fusion.31), channel_id=1, source_target_pairs={{0,48},{24,72},{48,96},{72,120},{96,144},{120,168},{144,192},{168,... | collective-permute-start | bytes 393224 | tf_op jit(solution)/shard_map/ppermute | solution.py:20
  33.3 4.6 %collective-permute-start.1 = (bf16[512,128]{0,1:T(8,128)(2,1)S(1)}, bf16[512,128]{0,1:T(8,128)(2,1)S(1)}, u32[]{:S(2)}, u32[]{:S(2)}) collective-permute-start(bf16[512,128]{0,1:T(8,128)(2,1)S(1)} %fusion.31), channel_id=1, source_target_pairs={{0,24},{24,48},{48,72},{72,96},{96,120},{120,144},{144,168},{168,1... | collective-permute-start | bytes 393224 | tf_op jit(solution)/shard_map/ppermute | solution.py:20
  37.9 15.5 %collective-permute-done = bf16[512,128]{0,1:T(8,128)(2,1)S(1)} collective-permute-done((bf16[512,128]{0,1:T(8,128)(2,1)S(1)}, bf16[512,128]{0,1:T(8,128)(2,1)S(1)}, u32[]{:S(2)}, u32[]{:S(2)}) %collective-permute-start) | collective-permute-done | bytes 131104 | tf_op jit(solution)/shard_map/ppermute | solution.py:20
  53.4 4.2 %collective-permute-done.1 = bf16[512,128]{0,1:T(8,128)(2,1)S(1)} collective-permute-done((bf16[512,128]{0,1:T(8,128)(2,1)S(1)}, bf16[512,128]{0,1:T(8,128)(2,1)S(1)}, u32[]{:S(2)}, u32[]{:S(2)}) %collective-permute-start.1) | collective-permute-done | bytes 131104 | tf_op jit(solution)/shard_map/ppermute | solution.py:20
  57.6 0.8 pad_maximum_fusion
  58.4 1.9 %collective-permute-start.2 = (bf16[1536,128]{0,1:T(8,128)(2,1)}, bf16[1536,128]{0,1:T(8,128)(2,1)}, u32[]{:S(2)}, u32[]{:S(2)}) collective-permute-start(bf16[1536,128]{0,1:T(8,128)(2,1)} %pad_maximum_fusion), channel_id=1, source_target_pairs={{0,1},{1,0},{2,3},{3,2},{4,5},{5,4},{6,7},{7,6},{8,9},{9,8},{10,11... | collective-permute-start | bytes 1179656 | tf_op jit(solution)/shard_map/ppermute | solution.py:82
  60.4 0.5 copy.27
  60.9 0.2 copy.45
  61.2 1.2 collective-permute-done.2
  62.4 2.3 %fusion.39 = (f32[512]{0:T(512)S(1)}, f32[512,1536]{1,0:T(8,128)S(1)}) fusion(bf16[1536,128]{0,1:T(8,128)(2,1)} %pad_maximum_fusion, bf16[1536,128]{0,1:T(8,128)(2,1)} %collective-permute-done.2, pred[]{:T(512)S(6)} %eq.3, f32[512,128]{0,1:T(8,128)S(1)} %get-tuple-element.15, f32[512,64]{0,1:T(8,128)S(1)} %get-tuple-element.22, ...), kind=kOutput, calls=%fused_computation.72 | convolution fusion | flops 207552000 | bytes 4730369 | tf_op jit(solution)/shard_map/dot_general | solution.py:97
  64.7 0.6 fusion.9
  65.3 1.7 %fusion.15 = bf16[512,128]{1,0:T(8,128)(2,1)S(1)} fusion(f32[512,1536]{1,0:T(8,128)S(1)} %get-tuple-element.24, f32[512]{0:T(512)S(1)} %fusion.9, f32[512]{0:T(512)S(1)} %get-tuple-element.23, bf16[1536,128]{0,1:T(8,128)(2,1)} %collective-permute-done.2, bf16[1536,128]{0,1:T(8,128)(2,1)} %pad_maximum_fusion, pred[]{:T(512)S(6)} %eq.3), kind=kOutput, calls=%fused_computation.26 | convolution fusion | flops 203948032 | bytes 4067329 | tf_op jit(solution)/shard_map/dot_general | solution.py:107
  67.0 0.3 broadcast_in_dim.8
  67.3 34.6 %all_to_all.26 = bf16[12,512,128]{2,1,0:T(8,128)(2,1)} all-to-all(bf16[12,512,128]{2,1,0:T(8,128)(2,1)S(1)} %broadcast_in_dim.8), channel_id=1, replica_groups=mesh['ctx'=32,'zl'=3,'x'=4,'core'=2] {'zl','x'}, dimensions={0} | all-to-all | bytes 3145728 | tf_op jit(solution)/shard_map/all_to_all | solution.py:113
  101.9 1.9 %collective-permute-start.3 = (bf16[12,512,128]{2,1,0:T(8,128)(2,1)}, bf16[12,512,128]{2,1,0:T(8,128)(2,1)}, u32[]{:S(2)}, u32[]{:S(2)}) collective-permute-start(bf16[12,512,128]{2,1,0:T(8,128)(2,1)} %all_to_all.26), channel_id=1, source_target_pairs={{0,1},{1,0},{2,3},{3,2},{4,5},{5,4},{6,7},{7,6},{8,9},{9,8},{10,11... | collective-permute-start | bytes 4718600 | tf_op jit(solution)/shard_map/ppermute | solution.py:114
  103.8 1.0 reshape.82
  104.8 3.3 %broadcast_select_fusion = (bf16[12,1,128,224]{2,1,0,3:T(2,128)(2,1)S(1)}, bf16[12,1,128,224]{2,1,0,3:T(2,128)(2,1)S(1)}) fusion(pred[]{:T(512)S(6)} %eq.3, bf16[12,2,128,224]{2,1,0,3:T(2,128)(2,1)S(1)} %reshape.82), kind=kLoop, calls=%fused_computation.19 | loop fusion | flops 688128 | bytes 2752513 | tf_op jit(solution)/shard_map/jit(_where)/select_n | solution.py:117
  108.1 2.0 %convolution_bitcast_fusion.1 = f32[512,224]{0,1:T(8,128)S(1)} fusion(bf16[12,512,128]{2,1,0:T(8,128)(2,1)} %all_to_all.26, bf16[12,1,128,224]{2,1,0,3:T(2,128)(2,1)S(1)} %get-tuple-element.14), kind=kOutput, calls=%fused_computation.24 | convolution fusion | flops 352321536 | bytes 2719744 | tf_op jit(solution)/shard_map/dot_general | solution.py:119
  110.2 2.1 %multiply_reduce_fusion = (f32[512]{0:T(512)S(1)}, f32[512,224]{0,1:T(8,128)S(1)}) fusion(f32[512,224]{0,1:T(8,128)S(1)} %convolution_bitcast_fusion.1, bf16[12,512,128]{2,1,0:T(8,128)(2,1)} %collective-permute-done.3, bf16[12,1,128,224]{2,1,0,3:T(2,128)(2,1)S(1)} %get-tuple-element.13), kind=kOutput, calls=%fused_computation.32 | convolution fusion | flops 352665088 | bytes 3180544 | tf_op jit(solution)/shard_map/dot_general | solution.py:121
  112.3 0.7 broadcast_in_dim.9
  112.9 4.5 %all-to-all-start.2 = ((f32[24,1,512]{2,1,0:T(1,128)}), f32[24,1,512]{2,1,0:T(1,128)S(1)}, u32[]{:S(2)}, u32[]{:S(2)}) async-start(f32[24,1,512]{2,1,0:T(1,128)} %broadcast_in_dim.9), calls=%async_computation.2 | async-start | bytes 98304 | tf_op jit(solution)/shard_map/all_to_all | solution.py:124
  117.4 1.1 constant_dynamic-slice_fusion
  118.6 0.1 copy.32
  118.7 5.8 %all-to-all-done.2 = f32[24,1,512]{2,1,0:T(1,128)S(1)} async-done(((f32[24,1,512]{2,1,0:T(1,128)}), f32[24,1,512]{2,1,0:T(1,128)S(1)}, u32[]{:S(2)}, u32[]{:S(2)}) %all-to-all-start.2) | async-done | bytes 49184 | tf_op jit(solution)/shard_map/all_to_all | solution.py:124
  124.6 0.8 add_convert_fusion
  (25 shorter events, 0.4 us)
Async XLA Ops:
  2.5 12.2 %copy-start.4 = (bf16[5376,128]{1,0:T(8,128)(2,1)S(1)}, bf16[5376,128]{1,0:T(8,128)(2,1)}, u32[]{:S(2)}) copy-start(bf16[5376,128]{1,0:T(8,128)(2,1)} %param.10) | copy-start | bytes 4128772
  2.5 12.2 %copy-start.5 = (f32[5376]{0:T(1024)S(1)}, f32[5376]{0:T(1024)}, u32[]{:S(2)}) copy-start(f32[5376]{0:T(1024)} %param.9) | copy-start | bytes 64516
  2.5 57.9 %all-to-all-start = ((bf16[128,24,224]{0,2,1:T(8,128)(2,1)}), bf16[128,24,224]{0,2,1:T(8,128)(2,1)S(1)}, u32[]{:S(2)}, u32[]{:S(2)}) async-start(bf16[128,24,224]{0,2,1:T(8,128)(2,1)} %bitcast), calls=%async_computation | async-start | bytes 2752512 | tf_op jit(solution)/shard_map/all_to_all | solution.py:76
  10.8 4.2 %copy-start = (bf16[512,5376]{1,0:T(8,128)(2,1)S(1)}, bf16[512,5376]{1,0:T(8,128)(2,1)}, u32[]{:S(2)}) copy-start(bf16[512,5376]{1,0:T(8,128)(2,1)} %param.8) | copy-start | bytes 16515076
  15.0 4.0 %copy-start.2 = (f32[128]{0:T(128)S(1)}, f32[128]{0:T(128)}, u32[]{:S(2)}) copy-start(f32[128]{0:T(128)} %param.12) | copy-start | bytes 1540
  15.0 4.0 %copy-start.3 = (f32[128]{0:T(128)S(1)}, f32[128]{0:T(128)}, u32[]{:S(2)}) copy-start(f32[128]{0:T(128)} %param.13) | copy-start | bytes 1540
  19.3 34.1 %collective-permute-start = (bf16[512,128]{0,1:T(8,128)(2,1)S(1)}, bf16[512,128]{0,1:T(8,128)(2,1)S(1)}, u32[]{:S(2)}, u32[]{:S(2)}) collective-permute-start(bf16[512,128]{0,1:T(8,128)(2,1)S(1)} %fusion.31), channel_id=1, source_target_pairs={{0,48},{24,72},{48,96},{72,120},{96,144},{120,168},{144,192},{168,... | collective-permute-start | bytes 393224 | tf_op jit(solution)/shard_map/ppermute | solution.py:20
  33.3 24.3 %collective-permute-start.1 = (bf16[512,128]{0,1:T(8,128)(2,1)S(1)}, bf16[512,128]{0,1:T(8,128)(2,1)S(1)}, u32[]{:S(2)}, u32[]{:S(2)}) collective-permute-start(bf16[512,128]{0,1:T(8,128)(2,1)S(1)} %fusion.31), channel_id=1, source_target_pairs={{0,24},{24,48},{48,72},{72,96},{96,120},{120,144},{144,168},{168,1... | collective-permute-start | bytes 393224 | tf_op jit(solution)/shard_map/ppermute | solution.py:20
  58.4 3.9 %collective-permute-start.2 = (bf16[1536,128]{0,1:T(8,128)(2,1)}, bf16[1536,128]{0,1:T(8,128)(2,1)}, u32[]{:S(2)}, u32[]{:S(2)}) collective-permute-start(bf16[1536,128]{0,1:T(8,128)(2,1)} %pad_maximum_fusion), channel_id=1, source_target_pairs={{0,1},{1,0},{2,3},{3,2},{4,5},{5,4},{6,7},{7,6},{8,9},{9,8},{10,11... | collective-permute-start | bytes 1179656 | tf_op jit(solution)/shard_map/ppermute | solution.py:82
  101.9 8.3 %collective-permute-start.3 = (bf16[12,512,128]{2,1,0:T(8,128)(2,1)}, bf16[12,512,128]{2,1,0:T(8,128)(2,1)}, u32[]{:S(2)}, u32[]{:S(2)}) collective-permute-start(bf16[12,512,128]{2,1,0:T(8,128)(2,1)} %all_to_all.26), channel_id=1, source_target_pairs={{0,1},{1,0},{2,3},{3,2},{4,5},{5,4},{6,7},{7,6},{8,9},{9,8},{10,11... | collective-permute-start | bytes 4718600 | tf_op jit(solution)/shard_map/ppermute | solution.py:114
  110.2 14.4 %copy-start.1 = (f32[224]{0:T(256)S(1)}, f32[224]{0:T(256)}, u32[]{:S(2)}) copy-start(f32[224]{0:T(256)} %param.15) | copy-start | bytes 2692
  112.9 11.6 %all-to-all-start.2 = ((f32[24,1,512]{2,1,0:T(1,128)}), f32[24,1,512]{2,1,0:T(1,128)S(1)}, u32[]{:S(2)}, u32[]{:S(2)}) async-start(f32[24,1,512]{2,1,0:T(1,128)} %broadcast_in_dim.9), calls=%async_computation.2 | async-start | bytes 98304 | tf_op jit(solution)/shard_map/all_to_all | solution.py:124
